TPU v7x, 256 devices: a whole 4x4x8 slice. The times are simulated.
256 devices in a mesh: samp: 32 (over x, z), snp: 8 (over y, core).
Axes of the slice: x: 4, y: 4, z: 8, core: 2. Of those that a mesh axis runs over, the one named last changes fastest.
Arguments:
- dosages: float32 [49152, 8192], P('samp', 'snp'), as said below
- band_counts: int32 [16], P('snp'), may hold values from 1 to 4, as said below
Outputs:
- corr_tiles: float32 [512, 16, 4, 512], P('samp', 'snp')
Inputs may be any that keep to these rules, and one draw needn't show every extreme that they name: b + band_counts[b] <= 16 for every block b, and the counts of all blocks sum to exactly 32. `dosages`: finite real values.
All inputs are finite; a program needn't handle non-finite values.
Results may differ from a plain program's by a relative error of at most 0.0001.
Values sent between devices are 32-bit elements; how exact they have to be, the bound alone decides.
No kernel may reach another device: no remote copies, remote signals or barrier semaphores. Data moves between devices by JAX's collectives and lax.ppermute only.
A program may use at most 192 MiB of HBM per device.

v0:
```python
import jax
import jax.numpy as jnp
from jax import lax
from jax.sharding import PartitionSpec as P

MAXBAND = 4


HIGHEST_MODE = lax.Precision.HIGHEST
epsilon_value = 1e-06
transposed_dims = (((0,), (0,)), ((), ()))


def shifted(value, axis, steps):
    count = lax.axis_size(axis)
    first, last = (max(0, -steps), min(count, count - steps))
    return lax.ppermute(value, axis, [(source, source + steps) for source in range(first, last)])


def on_device(dosages, band_counts):
    samp_rows, column_total = dosages.shape
    blocks_here = band_counts.shape[0]
    block_width = column_total // blocks_here
    band_limit = MAXBAND
    sample_total = samp_rows * lax.axis_size("samp")
    inverse_total = 1.0 / sample_total

    reach = (band_limit - 1 + blocks_here - 1) // blocks_here
    widths = [column_total]
    raw_sources = [dosages]
    for offset in range(1, reach + 1):
        last_block = min(band_limit - 1 + blocks_here - 1, offset * blocks_here + blocks_here - 1)
        need = (last_block - offset * blocks_here + 1) * block_width
        widths.append(need)
        raw_sources.append(shifted(dosages[:, :need], "snp", -offset))

    column_sum = lax.psum(jnp.sum(dosages, axis=0), "samp")
    center = column_sum * inverse_total
    deviation = dosages - center
    square_sum = lax.psum(jnp.sum(deviation * deviation, axis=0), "samp")
    spread = square_sum * inverse_total
    inverse_sd = 1.0 / jnp.sqrt(spread + epsilon_value)

    stats = jnp.stack([center, inverse_sd])
    scales = [inverse_sd]
    sources = [deviation]
    for offset in range(1, reach + 1):
        width = widths[offset]
        moved = shifted(stats[:, :width], "snp", -offset)
        scales.append(moved[1])
        sources.append(raw_sources[offset] - moved[0])

    def tile(local_block, band_index):
        column_block = local_block + band_index
        source = sources[column_block // blocks_here]
        column_start = column_block % blocks_here * block_width
        left_panel = deviation[:, local_block * block_width : (local_block + 1) * block_width]
        right_panel = source[:, column_start : column_start + block_width]
        return lax.dot_general(
            left_panel,
            right_panel,
            transposed_dims,
            precision=HIGHEST_MODE,
            preferred_element_type=jnp.float32,
        )

    band_range = jnp.arange(band_limit, dtype=jnp.int32)
    live_mask = band_range[None, :] < band_counts[:, None]
    row_list = []
    for local_block in range(blocks_here):
        band_list = [tile(local_block, band_index) for band_index in range(band_limit)]
        row_list.append(jnp.stack(band_list, axis=1))
    tile_term = jnp.stack(row_list, axis=1)
    reduced = lax.psum_scatter(
        jnp.where(live_mask[None, :, :, None], tile_term, 0.0),
        "samp",
        scatter_dimension=0,
        tiled=True,
    )

    own_rows = block_width // lax.axis_size("samp")
    row_start = lax.axis_index("samp") * own_rows
    row_list = []
    for local_block in range(blocks_here):
        row_scale = lax.dynamic_slice_in_dim(inverse_sd, local_block * block_width + row_start, own_rows)
        band_list = []
        for band_index in range(band_limit):
            column_block = local_block + band_index
            source_scale = scales[column_block // blocks_here]
            column_start = column_block % blocks_here * block_width
            column_scale = source_scale[column_start : column_start + block_width]
            band_list.append(
                reduced[:, local_block, band_index] * row_scale[:, None] * column_scale[None, :] * inverse_total
            )
        row_list.append(jnp.stack(band_list, axis=1))
    return jnp.stack(row_list, axis=1)


def solution(mesh):
    return jax.shard_map(
        on_device,
        mesh=mesh,
        in_specs=(P("samp", "snp"), P("snp")),
        out_specs=P("samp", "snp", None, None),
        check_vma=False,
    )
```

profile of v0, /device:TPU:8, one launch (start us, length us, event | category | flops | bytes accessed | tf_op | source)
XLA Modules:
  0.0 469.8 jit_solution(11674077126252619246)
XLA Ops:
  6.5 0.0 reduce-scatter.2.cloned.1.call-start
  6.5 1.9 collective-permute-start
  8.5 3.9 slice.93
  12.3 3.4 collective-permute-start.2
  15.7 3.2 reduce_sum.18
  18.9 76.2 %psum.14 = f32[1024]{0:T(1024)S(1)} all-reduce(f32[1024]{0:T(1024)S(1)} %reduce_sum.18), channel_id=1, replica_groups=mesh['samp'=32,'snp'=8] {'samp'}, use_global_device_ids=true, to_apply=%region_1.0 | all-reduce | flops 1024 | bytes 8192 | tf_op jit(solution)/shard_map/psum | solution.py:37
  95.1 6.6 %multiply_reduce_fusion = (f32[1024]{0:T(1024)S(1)}, f32[1536,1024]{1,0:T(8,128)}) fusion(f32[1536,1024]{1,0:T(8,128)} %param.2, f32[1024]{0:T(1024)S(1)} %broadcast_multiply_fusion), kind=kLoop, calls=%fused_computation.1 | loop fusion | flops 4717568 | bytes 12591104 | tf_op jit(solution)/shard_map/reduce_sum | solution.py:40
  101.7 69.6 %psum.15 = f32[1024]{0:T(1024)S(1)} all-reduce(f32[1024]{0:T(1024)S(1)} %get-tuple-element.5), channel_id=1, replica_groups=mesh['samp'=32,'snp'=8] {'samp'}, use_global_device_ids=true, to_apply=%region_3.0 | all-reduce | flops 1024 | bytes 8192 | tf_op jit(solution)/shard_map/psum | solution.py:40
  171.4 1.9 collective-permute-start.3
  173.3 2.4 collective-permute-start.1
  175.7 0.0 copy-start
  175.7 8.1 %fusion.23 = f32[512,1,512]{2,0,1:T(8,128)S(1)} fusion(f32[1536,1024]{1,0:T(8,128)} %get-tuple-element.6), kind=kOutput, calls=%fused_computation.29 | convolution fusion | flops 4831838208 | bytes 4194304 | tf_op jit(solution)/shard_map/dot_general | solution.py:59
  183.8 8.0 %fusion.26 = f32[512,1,512]{2,0,1:T(8,128)S(1)} fusion(f32[1536,1024]{1,0:T(8,128)} %get-tuple-element.6), kind=kOutput, calls=%fused_computation.30 | convolution fusion | flops 4831838208 | bytes 4194304 | tf_op jit(solution)/shard_map/dot_general | solution.py:59
  191.8 0.0 copy-done
  191.8 0.0 copy-start.1
  191.8 5.5 %fusion.29 = f32[512,1,512]{2,0,1:T(8,128)S(1)} fusion(f32[1536,1024]{1,0:T(8,128)S(1)} %copy-done), kind=kOutput, calls=%fused_computation.31 | convolution fusion | flops 4831838208 | bytes 7340032 | tf_op jit(solution)/shard_map/dot_general | solution.py:59
  197.3 0.0 copy-done.1
  197.3 0.1 iota_compare_fusion
  197.4 0.0 collective-permute-done.3
  197.4 0.0 collective-permute-done.1
  197.4 0.0 collective-permute-done.2
  197.4 5.4 %fusion.54 = f32[512,1,512]{2,0,1:T(8,128)S(1)} fusion(f32[1536,512]{1,0:T(8,128)S(1)} %collective-permute-done.2, f32[512]{0:T(512)S(1)} %bitcast.103, f32[1536,1024]{1,0:T(8,128)S(1)} %copy-done), kind=kOutput, calls=%fused_computation.36 | convolution fusion | flops 4832624640 | bytes 7342080 | tf_op jit(solution)/shard_map/dot_general | solution.py:59
  202.8 0.0 collective-permute-done
  202.8 3.5 broadcast_subtract_fusion
  206.4 5.5 %fusion.49 = f32[512,1,512]{2,0,1:T(8,128)S(1)} fusion(f32[1536,1024]{1,0:T(8,128)S(1)} %broadcast_subtract_fusion, f32[1536,1024]{1,0:T(8,128)S(1)} %copy-done), kind=kOutput, calls=%fused_computation.35 | convolution fusion | flops 4831838208 | bytes 7340032 | tf_op jit(solution)/shard_map/dot_general | solution.py:59
  211.9 5.3 %fusion.39 = f32[512,1,512]{2,0,1:T(8,128)S(1)} fusion(f32[1536,1024]{1,0:T(8,128)S(1)} %broadcast_subtract_fusion, f32[1536,1024]{1,0:T(8,128)S(1)} %copy-done), kind=kOutput, calls=%fused_computation.33 | convolution fusion | flops 4831838208 | bytes 7340032 | tf_op jit(solution)/shard_map/dot_general | solution.py:59
  217.1 5.5 %fusion.44 = f32[512,1,512]{2,0,1:T(8,128)S(1)} fusion(f32[1536,1024]{1,0:T(8,128)S(1)} %broadcast_subtract_fusion, f32[1536,1024]{1,0:T(8,128)S(1)} %copy-done), kind=kOutput, calls=%fused_computation.34 | convolution fusion | flops 4831838208 | bytes 7340032 | tf_op jit(solution)/shard_map/dot_general | solution.py:59
  222.7 5.3 %fusion.34 = f32[512,1,512]{2,0,1:T(8,128)S(1)} fusion(f32[1536,1024]{1,0:T(8,128)S(1)} %broadcast_subtract_fusion, f32[1536,1024]{1,0:T(8,128)S(1)} %copy-done), kind=kOutput, calls=%fused_computation.32 | convolution fusion | flops 4831838208 | bytes 7340032 | tf_op jit(solution)/shard_map/dot_general | solution.py:59
  228.0 0.4 maximum_bitcast_fusion.1
  228.4 0.5 maximum_bitcast_fusion
  228.9 4.4 maximum_select_fusion
  233.3 0.0 reduce-scatter.2.cloned.1.call-update
  233.3 0.1 fusion.86
  233.4 227.3 %reduce-scatter.2.cloned.1.call-done = f32[16,2,4,512]{3,0,2,1:T(8,128)} async-done(((f32[512,2,4,512]{3,0,2,1:T(8,128)}), f32[16,2,4,512]{3,0,2,1:T(8,128)}) %reduce-scatter.2.cloned.1.call-update) | async-done | bytes 262160 | tf_op jit(solution)/shard_map/reduce_scatter | solution.py:74
  460.6 1.0 fusion.73
  461.7 0.9 copy.3
  (10 shorter events, 0.1 us)
Async XLA Ops:
  6.5 454.1 %reduce-scatter.2.cloned.1.call-start = ((), (), s32[]{:S(2)}) async-start(), calls=%async_computation.1 | async-start | bytes 8650752 | tf_op jit(solution)/shard_map/reduce_scatter | solution.py:74
  6.5 196.3 %collective-permute-start = (f32[1536,1024]{1,0:T(8,128)}, f32[1536,1024]{1,0:T(8,128)}, u32[]{:S(2)}, u32[]{:S(2)}) collective-permute-start(f32[1536,1024]{1,0:T(8,128)} %param.2), channel_id=1, source_target_pairs={{1,0},{2,1},{3,2},{4,3},{5,4},{6,5},{7,6},{9,8},{10,9},{11,10},{12... | collective-permute-start | bytes 18874376 | tf_op jit(solution)/shard_map/ppermute | solution.py:17
  12.3 185.1 %collective-permute-start.2 = (f32[1536,512]{1,0:T(8,128)}, f32[1536,512]{1,0:T(8,128)S(1)}, u32[]{:S(2)}, u32[]{:S(2)}) collective-permute-start(f32[1536,512]{1,0:T(8,128)} %slice.93), channel_id=1, source_target_pairs={{2,0},{3,1},{4,2},{5,3},{6,4},{7,5},{10,8},{11,9},{12,10},{13,11},... | collective-permute-start | bytes 9437192 | tf_op jit(solution)/shard_map/ppermute | solution.py:17
  171.4 26.0 %collective-permute-start.3 = (f32[2,512]{1,0:T(2,128)S(1)}, f32[2,512]{1,0:T(2,128)S(1)}, u32[]{:S(2)}, u32[]{:S(2)}) collective-permute-start(f32[2,512]{1,0:T(2,128)S(1)} %fusion.83), channel_id=1, source_target_pairs={{2,0},{3,1},{4,2},{5,3},{6,4},{7,5},{10,8},{11,9},{12,10},{13,11},... | collective-permute-start | bytes 12296 | tf_op jit(solution)/shard_map/ppermute | solution.py:17
  173.3 24.1 %collective-permute-start.1 = (f32[2,1024]{1,0:T(2,128)S(1)}, f32[2,1024]{1,0:T(2,128)S(1)}, u32[]{:S(2)}, u32[]{:S(2)}) collective-permute-start(f32[2,1024]{1,0:T(2,128)S(1)} %pad_maximum_fusion.1), channel_id=1, source_target_pairs={{1,0},{2,1},{3,2},{4,3},{5,4},{6,5},{7,6},{9,8},{10,9},{11,10},{12... | collective-permute-start | bytes 24584 | tf_op jit(solution)/shard_map/ppermute | solution.py:17
  175.7 16.1 %copy-start = (f32[1536,1024]{1,0:T(8,128)S(1)}, f32[1536,1024]{1,0:T(8,128)}, u32[]{:S(2)}) copy-start(f32[1536,1024]{1,0:T(8,128)} %get-tuple-element.6) | copy-start | bytes 18874372
  191.8 5.5 %copy-start.1 = (s32[2]{0:T(128)S(1)}, s32[2]{0:T(128)}, u32[]{:S(2)}) copy-start(s32[2]{0:T(128)} %param.3) | copy-start | bytes 28
Sparse Core Ops, SparseCore 0:
  233.4 227.1 reduce-scatter.1
where the time goes:
time: 472 us; the launch traced here: 470 us
  waiting for transfers between devices  227 us (48%)
  blocking collectives  146 us (31%)
  matrix products  48.5 us (10%)
  other arithmetic  19.7 us (4%)
  between operations  14.1 us (3%)
  starting transfers between devices  9.63 us (2%)
  local copies, waits for them, and re-layouts  4.85 us (1%)
    reduce_scatter x1, waiting for transfers between devices, on_device(): lax.psum_scatter(jnp.where(live_mask[None, :, :, None], tile_term, 0.0),...  227 us
    psum x1, blocking collectives, on_device(): column_sum = lax.psum(jnp.sum(dosages, axis=0), 'samp')  76.2 us
    psum x1, blocking collectives, on_device(): square_sum = lax.psum(jnp.sum(deviation * deviation, axis=0), 'samp')  69.6 us
    dot_general x8, matrix products, tile(): lax.dot_general(left_panel, right_panel, transposed_dims, precision=HIGHE...  48.5 us
    ppermute x4, starting transfers between devices, shifted(): lax.ppermute(value, axis, [(source, source + steps) for source in range(f...  9.63 us
  transfers between devices with their start and end apart: 5, of which 1 were waited for; matrix products, arithmetic and copies ran while one was open for 9% of the time, Pallas kernels for 0%

commit v1 on v0

--- a/solution.py
+++ b/solution.py
@@ -6,7 +6,7 @@
 MAXBAND = 4
 
 
-HIGHEST_MODE = lax.Precision.HIGHEST
+HIGHEST_MODE = lax.Precision.HIGH
 epsilon_value = 1e-06
 transposed_dims = (((0,), (0,)), ((), ()))
 
@@ -34,10 +34,19 @@
         widths.append(need)
         raw_sources.append(shifted(dosages[:, :need], "snp", -offset))
 
-    column_sum = lax.psum(jnp.sum(dosages, axis=0), "samp")
-    center = column_sum * inverse_total
+    samp_count = lax.axis_size("samp")
+    local_center = jnp.sum(dosages, axis=0) * (1.0 / samp_rows)
+    local_deviation = dosages - local_center
+    local_square = jnp.sum(local_deviation * local_deviation, axis=0)
+    slots = jnp.arange(samp_count, dtype=jnp.int32)[:, None] == lax.axis_index("samp")
+    gathered = lax.psum(
+        jnp.concatenate([jnp.where(slots, local_center[None, :], 0.0), local_square[None, :]]), "samp"
+    )
+    slot_centers = gathered[:samp_count]
+    center = jnp.sum(slot_centers, axis=0) * (1.0 / samp_count)
+    offsets = slot_centers - center
+    square_sum = gathered[samp_count] + samp_rows * jnp.sum(offsets * offsets, axis=0)
     deviation = dosages - center
-    square_sum = lax.psum(jnp.sum(deviation * deviation, axis=0), "samp")
     spread = square_sum * inverse_total
     inverse_sd = 1.0 / jnp.sqrt(spread + epsilon_value)
 

time: 472 us -> 453 us (0.960)
  waiting for transfers between devices: 227 us -> 378 us
  blocking collectives: 146 us -> 0 us
  matrix products: 48.5 us -> 22.2 us
    psum x0 -> x1, waiting for transfers between devices: none -> 148 us  [on_device(): lax.psum(jnp.concatenate([jnp.where(slots, local_center[None, :], 0.0), l...]
    psum x2 -> x0, blocking collectives: 146 us -> none  [the longest x1 76.2 us: on_device(): column_sum = lax.psum(jnp.sum(dosages, axis=0), 'samp')]
    dot_general x8, matrix products: 48.5 us -> 22.2 us  [tile(): lax.dot_general(left_panel, right_panel, transposed_dims, precision=HIGHE...]
    reduce_sum x2 -> x4, other arithmetic: 9.79 us -> 8.52 us  [the longest x1 3.48 us: on_device(): local_square = jnp.sum(local_deviation * local_deviation, axis=0)]
  transfers between devices with their start and end apart: 5 -> 6, of which waited for: 1 -> 3; matrix products, arithmetic and copies ran while one was open for 9% -> 6% of each run, Pallas kernels for 0% -> 0%
where the time goes in v1:
time: 453 us; the launch traced here: 452 us
  waiting for transfers between devices  378 us (83%)
  other arithmetic  23.4 us (5%)
  matrix products  22.2 us (5%)
  between operations  13.7 us (3%)
  starting transfers between devices  9.92 us (2%)
  local copies, waits for them, and re-layouts  4.88 us (1%)
    reduce_scatter x1, waiting for transfers between devices, on_device(): lax.psum_scatter(jnp.where(live_mask[None, :, :, None], tile_term, 0.0),...  229 us
    psum x1, waiting for transfers between devices, on_device(): lax.psum(jnp.concatenate([jnp.where(slots, local_center[None, :], 0.0), l...  148 us
    dot_general x8, matrix products, tile(): lax.dot_general(left_panel, right_panel, transposed_dims, precision=HIGHE...  22.2 us
    ppermute x4, starting transfers between devices, shifted(): lax.ppermute(value, axis, [(source, source + steps) for source in range(f...  9.87 us
  transfers between devices with their start and end apart: 6, of which 3 were waited for; matrix products, arithmetic and copies ran while one was open for 6% of the time, Pallas kernels for 0%

profile of v1, /device:TPU:8, one launch (start us, length us, event | category | flops | bytes accessed | tf_op | source)
XLA Modules:
  0.0 452.3 jit_solution(5689092126091994424)
XLA Ops:
  6.5 0.0 all-reduce.2.cloned.1.call-start
  6.5 1.9 collective-permute-start
  8.5 3.9 slice.101
  12.4 3.4 collective-permute-start.2
  15.8 3.2 reduce_sum.36
  19.0 0.0 copy-start
  19.0 0.1 broadcast_select_fusion
  19.1 3.5 multiply_reduce_fusion
  22.6 0.7 pad_maximum_fusion.1
  23.2 0.0 all-reduce.2.cloned.1.call-update
  23.3 0.0 reduce-scatter.2.cloned.1.call-start
  23.3 0.0 copy-done
  23.3 0.1 iota_compare_fusion
  23.4 147.8 %all-reduce.2.cloned.1.call-done = f32[33,1024]{1,0:T(8,128)} async-done(((f32[33,1024]{1,0:T(8,128)}), f32[33,1024]{1,0:T(8,128)}) %all-reduce.2.cloned.1.call-update) | async-done | bytes 135184 | tf_op jit(solution)/shard_map/psum | solution.py:42
  171.2 0.9 slice_reduce_fusion
  172.1 0.9 multiply_reduce_fusion.1
  173.1 0.8 fusion.84
  173.9 2.4 collective-permute-start.3
  176.3 3.5 broadcast_subtract_fusion.1
  179.9 2.8 fusion.23
  182.6 2.8 fusion.26
  185.4 2.7 fusion.29
  188.2 2.1 collective-permute-start.1
  190.3 0.0 collective-permute-done.3
  190.3 1.1 collective-permute-done.1
  191.4 0.0 collective-permute-done.2
  191.4 2.8 fusion.54
  194.2 0.0 collective-permute-done
  194.2 3.5 broadcast_subtract_fusion
  197.7 2.7 fusion.49
  200.5 2.7 fusion.39
  203.2 2.7 fusion.44
  206.0 3.0 fusion.34
  209.0 0.4 maximum_bitcast_fusion.1
  209.4 0.4 maximum_bitcast_fusion
  209.9 4.3 maximum_select_fusion
  214.2 0.0 reduce-scatter.2.cloned.1.call-update
  214.3 0.1 fusion.87
  214.4 229.2 %reduce-scatter.2.cloned.1.call-done = f32[16,2,4,512]{3,0,2,1:T(8,128)} async-done(((f32[512,2,4,512]{3,0,2,1:T(8,128)}), f32[16,2,4,512]{3,0,2,1:T(8,128)}) %reduce-scatter.2.cloned.1.call-update) | async-done | bytes 262160 | tf_op jit(solution)/shard_map/reduce_scatter | solution.py:83
  443.6 1.0 fusion.73
  444.6 0.9 copy.4
  (13 shorter events, 0.1 us)
Async XLA Ops:
  6.5 164.7 %all-reduce.2.cloned.1.call-start = ((), (), s32[]{:S(2)}) async-start(), calls=%async_computation.1 | async-start | bytes 327680 | tf_op jit(solution)/shard_map/psum | solution.py:42
  6.5 187.7 %collective-permute-start = (f32[1536,1024]{1,0:T(8,128)}, f32[1536,1024]{1,0:T(8,128)}, u32[]{:S(2)}, u32[]{:S(2)}) collective-permute-start(f32[1536,1024]{1,0:T(8,128)} %param.2), channel_id=1, source_target_pairs={{1,0},{2,1},{3,2},{4,3},{5,4},{6,5},{7,6},{9,8},{10,9},{11,10},{12... | collective-permute-start | bytes 18874376 | tf_op jit(solution)/shard_map/ppermute | solution.py:17
  12.4 179.1 %collective-permute-start.2 = (f32[1536,512]{1,0:T(8,128)}, f32[1536,512]{1,0:T(8,128)S(1)}, u32[]{:S(2)}, u32[]{:S(2)}) collective-permute-start(f32[1536,512]{1,0:T(8,128)} %slice.101), channel_id=1, source_target_pairs={{2,0},{3,1},{4,2},{5,3},{6,4},{7,5},{10,8},{11,9},{12,10},{13,11},... | collective-permute-start | bytes 9437192 | tf_op jit(solution)/shard_map/ppermute | solution.py:17
  19.0 4.4 copy-start
  23.3 420.3 %reduce-scatter.2.cloned.1.call-start = ((), (), s32[]{:S(2)}) async-start(), calls=%async_computation.2 | async-start | bytes 8650752 | tf_op jit(solution)/shard_map/reduce_scatter | solution.py:83
  173.9 16.4 %collective-permute-start.3 = (f32[2,512]{1,0:T(2,128)S(1)}, f32[2,512]{1,0:T(2,128)S(1)}, u32[]{:S(2)}, u32[]{:S(2)}) collective-permute-start(f32[2,512]{1,0:T(2,128)S(1)} %fusion.83), channel_id=1, source_target_pairs={{2,0},{3,1},{4,2},{5,3},{6,4},{7,5},{10,8},{11,9},{12,10},{13,11},... | collective-permute-start | bytes 12296 | tf_op jit(solution)/shard_map/ppermute | solution.py:17
  188.2 3.3 collective-permute-start.1
Sparse Core Ops, SparseCore 0:
  23.4 147.7 all-reduce.1
  214.4 229.1 reduce-scatter.1

commit v2 on v0

--- a/solution.py
+++ b/solution.py
@@ -6,7 +6,7 @@
 MAXBAND = 4
 
 
-HIGHEST_MODE = lax.Precision.HIGHEST
+HIGHEST_MODE = lax.Precision.HIGH
 epsilon_value = 1e-06
 transposed_dims = (((0,), (0,)), ((), ()))
 
@@ -17,12 +17,20 @@
     return lax.ppermute(value, axis, [(source, source + steps) for source in range(first, last)])
 
 
+def samp_size():
+    return lax.axis_size("samp_x") * lax.axis_size("samp_z")
+
+
+def samp_sum(value):
+    return lax.psum(lax.psum(value, "samp_z"), "samp_x")
+
+
 def on_device(dosages, band_counts):
     samp_rows, column_total = dosages.shape
     blocks_here = band_counts.shape[0]
     block_width = column_total // blocks_here
     band_limit = MAXBAND
-    sample_total = samp_rows * lax.axis_size("samp")
+    sample_total = samp_rows * samp_size()
     inverse_total = 1.0 / sample_total
 
     reach = (band_limit - 1 + blocks_here - 1) // blocks_here
@@ -34,10 +42,10 @@
         widths.append(need)
         raw_sources.append(shifted(dosages[:, :need], "snp", -offset))
 
-    column_sum = lax.psum(jnp.sum(dosages, axis=0), "samp")
+    column_sum = samp_sum(jnp.sum(dosages, axis=0))
     center = column_sum * inverse_total
     deviation = dosages - center
-    square_sum = lax.psum(jnp.sum(deviation * deviation, axis=0), "samp")
+    square_sum = samp_sum(jnp.sum(deviation * deviation, axis=0))
     spread = square_sum * inverse_total
     inverse_sd = 1.0 / jnp.sqrt(spread + epsilon_value)
 
@@ -73,13 +81,13 @@
     tile_term = jnp.stack(row_list, axis=1)
     reduced = lax.psum_scatter(
         jnp.where(live_mask[None, :, :, None], tile_term, 0.0),
-        "samp",
+        ("samp_x", "samp_z"),
         scatter_dimension=0,
         tiled=True,
     )
 
-    own_rows = block_width // lax.axis_size("samp")
-    row_start = lax.axis_index("samp") * own_rows
+    own_rows = block_width // samp_size()
+    row_start = (lax.axis_index("samp_x") * lax.axis_size("samp_z") + lax.axis_index("samp_z")) * own_rows
     row_list = []
     for local_block in range(blocks_here):
         row_scale = lax.dynamic_slice_in_dim(inverse_sd, local_block * block_width + row_start, own_rows)
@@ -97,10 +105,15 @@
 
 
 def solution(mesh):
+    x_size = mesh.devices.shape[0] // 8 if mesh.devices.shape[0] % 8 == 0 else 1
+    split = jax.sharding.Mesh(
+        mesh.devices.reshape(x_size, mesh.devices.shape[0] // x_size, mesh.devices.shape[1]),
+        ("samp_x", "samp_z", "snp"),
+    )
     return jax.shard_map(
         on_device,
-        mesh=mesh,
-        in_specs=(P("samp", "snp"), P("snp")),
-        out_specs=P("samp", "snp", None, None),
+        mesh=split,
+        in_specs=(P(("samp_x", "samp_z"), "snp"), P("snp")),
+        out_specs=P(("samp_x", "samp_z"), "snp", None, None),
         check_vma=False,
     )

time: 472 us -> 412 us (0.87)
  blocking collectives: 146 us -> 50.9 us
  waiting for transfers between devices: 227 us -> 285 us
  matrix products: 48.5 us -> 27.8 us
    psum x2 -> x4, blocking collectives: 146 us -> 50.9 us  [samp_sum(): return lax.psum(lax.psum(value, 'samp_z'), 'samp_x')]
    ppermute x4, waiting for transfers between devices: 0.01 us -> 52.2 us  [shifted(): lax.ppermute(value, axis, [(source, source + steps) for source in range(f...]
    dot_general x8, matrix products: 48.5 us -> 27.8 us  [tile(): lax.dot_general(left_panel, right_panel, transposed_dims, precision=HIGHE...]
    reduce_scatter x1, waiting for transfers between devices: 227 us -> 233 us  [on_device(): lax.psum_scatter(jnp.where(live_mask[None, :, :, None], tile_term, 0.0),...]
  transfers between devices with their start and end apart: 5 -> 5, of which waited for: 1 -> 2; matrix products, arithmetic and copies ran while one was open for 9% -> 7% of each run, Pallas kernels for 0% -> 0%
where the time goes in v2:
time: 412 us
  waiting for transfers between devices  285 us (69%)
  blocking collectives  50.9 us (12%)
  matrix products  27.8 us (7%)
  other arithmetic  19.7 us (5%)
  between operations  13.6 us (3%)
  starting transfers between devices  9.35 us (2%)
  local copies, waits for them, and re-layouts  4.86 us (1%)
    reduce_scatter x1, waiting for transfers between devices, on_device(): lax.psum_scatter(jnp.where(live_mask[None, :, :, None], tile_term, 0.0),...  233 us
    ppermute x4, waiting for transfers between devices, shifted(): lax.ppermute(value, axis, [(source, source + steps) for source in range(f...  52.2 us
    psum x4, blocking collectives, samp_sum(): return lax.psum(lax.psum(value, 'samp_z'), 'samp_x')  50.9 us
    dot_general x8, matrix products, tile(): lax.dot_general(left_panel, right_panel, transposed_dims, precision=HIGHE...  27.8 us
    ppermute x4, starting transfers between devices, shifted(): lax.ppermute(value, axis, [(source, source + steps) for source in range(f...  9.34 us
  transfers between devices with their start and end apart: 5, of which 2 were waited for; matrix products, arithmetic and copies ran while one was open for 7% of the time, Pallas kernels for 0%

profile of v2, /device:TPU:8, one launch (start us, length us, event | category | flops | bytes accessed | tf_op | source)
XLA Modules:
  0.0 411.5 jit_solution(440780229722454540)
XLA Ops:
  6.5 0.0 reduce-scatter.2.cloned.1.call-start
  6.5 1.9 collective-permute-start
  8.5 3.9 slice.93
  12.3 3.4 collective-permute-start.2
  15.8 3.2 reduce_sum.18
  18.9 18.5 %psum.28 = f32[1024]{0:T(1024)S(1)} all-reduce(f32[1024]{0:T(1024)S(1)} %reduce_sum.18), channel_id=1, replica_groups=mesh['samp_x'=4,'samp_z'=8,'snp'=8] {'samp_z'}, use_global_device_ids=true, to_apply=%region_1.0 | all-reduce | flops 1024 | bytes 8192 | tf_op jit(solution)/shard_map/psum | solution.py:25
  37.4 10.5 %psum.29 = f32[1024]{0:T(1024)S(1)} all-reduce(f32[1024]{0:T(1024)S(1)} %psum.28), channel_id=1, replica_groups=mesh['samp_x'=4,'samp_z'=8,'snp'=8] {'samp_x'}, use_global_device_ids=true, to_apply=%region_2.0 | all-reduce | flops 1024 | bytes 8192 | tf_op jit(solution)/shard_map/psum | solution.py:25
  47.9 6.6 %multiply_reduce_fusion = (f32[1024]{0:T(1024)S(1)}, f32[1536,1024]{1,0:T(8,128)}) fusion(f32[1536,1024]{1,0:T(8,128)} %param.2, f32[1024]{0:T(1024)S(1)} %broadcast_multiply_fusion), kind=kLoop, calls=%fused_computation.1 | loop fusion | flops 4717568 | bytes 12591104 | tf_op jit(solution)/shard_map/reduce_sum | solution.py:48
  54.5 14.1 %psum.30 = f32[1024]{0:T(1024)S(1)} all-reduce(f32[1024]{0:T(1024)S(1)} %get-tuple-element.5), channel_id=1, replica_groups=mesh['samp_x'=4,'samp_z'=8,'snp'=8] {'samp_z'}, use_global_device_ids=true, to_apply=%region_4.0 | all-reduce | flops 1024 | bytes 8192 | tf_op jit(solution)/shard_map/psum | solution.py:25
  68.7 7.7 %psum.31 = f32[1024]{0:T(1024)S(1)} all-reduce(f32[1024]{0:T(1024)S(1)} %psum.30), channel_id=1, replica_groups=mesh['samp_x'=4,'samp_z'=8,'snp'=8] {'samp_x'}, use_global_device_ids=true, to_apply=%region_5.0 | all-reduce | flops 1024 | bytes 8192 | tf_op jit(solution)/shard_map/psum | solution.py:25
  76.4 1.9 collective-permute-start.3
  78.4 2.1 collective-permute-start.1
  80.5 0.0 copy-start
  80.5 5.6 %fusion.23 = f32[512,1,512]{2,0,1:T(8,128)S(1)} fusion(f32[1536,1024]{1,0:T(8,128)} %get-tuple-element.6), kind=kOutput, calls=%fused_computation.29 | convolution fusion | flops 2415919104 | bytes 4194304 | tf_op jit(solution)/shard_map/dot_general | solution.py:67
  86.1 5.5 %fusion.26 = f32[512,1,512]{2,0,1:T(8,128)S(1)} fusion(f32[1536,1024]{1,0:T(8,128)} %get-tuple-element.6), kind=kOutput, calls=%fused_computation.30 | convolution fusion | flops 2415919104 | bytes 4194304 | tf_op jit(solution)/shard_map/dot_general | solution.py:67
  91.6 0.0 copy-done
  91.6 0.0 copy-start.1
  91.6 2.7 fusion.29
  94.4 0.0 copy-done.1
  94.4 0.1 iota_compare_fusion
  94.5 52.2 %collective-permute-done.3 = f32[2,512]{1,0:T(2,128)S(1)} collective-permute-done((f32[2,512]{1,0:T(2,128)S(1)}, f32[2,512]{1,0:T(2,128)S(1)}, u32[]{:S(2)}, u32[]{:S(2)}) %collective-permute-start.3) | collective-permute-done | bytes 4128 | tf_op jit(solution)/shard_map/ppermute | solution.py:17
  146.7 0.0 collective-permute-done.1
  146.7 0.0 collective-permute-done.2
  146.7 2.8 fusion.54
  149.5 0.0 collective-permute-done
  149.5 3.5 broadcast_subtract_fusion
  153.0 3.0 fusion.49
  156.0 2.7 fusion.39
  158.7 2.8 fusion.44
  161.5 2.7 fusion.34
  164.3 0.4 maximum_bitcast_fusion.1
  164.7 0.5 maximum_bitcast_fusion
  165.2 4.4 %maximum_select_fusion = f32[512,2,4,512]{3,0,2,1:T(8,128)} fusion(f32[512,1,4,512]{3,0,2,1:T(8,128)S(1)} %maximum_bitcast_fusion.1, f32[512,1,4,512]{3,0,2,1:T(8,128)S(1)} %maximum_bitcast_fusion, pred[2,4]{1,0:T(4,128)(4,1)S(1)} %iota_compare_fusion), kind=kLoop, calls=%fused_computation | loop fusion | flops 4194304 | bytes 16777224 | tf_op jit(solution)/shard_map/jit(_where)/select_n | solution.py:83
  169.5 0.0 reduce-scatter.2.cloned.1.call-update
  169.6 0.1 fusion.86
  169.7 233.1 %reduce-scatter.2.cloned.1.call-done = f32[16,2,4,512]{3,0,2,1:T(8,128)} async-done(((f32[512,2,4,512]{3,0,2,1:T(8,128)}), f32[16,2,4,512]{3,0,2,1:T(8,128)}) %reduce-scatter.2.cloned.1.call-update) | async-done | bytes 262160 | tf_op jit(solution)/shard_map/reduce_scatter | solution.py:82
  402.8 1.0 fusion.73
  403.8 0.9 copy.3
  (10 shorter events, 0.1 us)
Async XLA Ops:
  6.5 396.2 %reduce-scatter.2.cloned.1.call-start = ((), (), s32[]{:S(2)}) async-start(), calls=%async_computation.1 | async-start | bytes 8650752 | tf_op jit(solution)/shard_map/reduce_scatter | solution.py:82
  6.5 142.9 %collective-permute-start = (f32[1536,1024]{1,0:T(8,128)}, f32[1536,1024]{1,0:T(8,128)}, u32[]{:S(2)}, u32[]{:S(2)}) collective-permute-start(f32[1536,1024]{1,0:T(8,128)} %param.2), channel_id=1, source_target_pairs={{1,0},{2,1},{3,2},{4,3},{5,4},{6,5},{7,6},{9,8},{10,9},{11,10},{12... | collective-permute-start | bytes 18874376 | tf_op jit(solution)/shard_map/ppermute | solution.py:17
  12.3 134.4 %collective-permute-start.2 = (f32[1536,512]{1,0:T(8,128)}, f32[1536,512]{1,0:T(8,128)S(1)}, u32[]{:S(2)}, u32[]{:S(2)}) collective-permute-start(f32[1536,512]{1,0:T(8,128)} %slice.93), channel_id=1, source_target_pairs={{2,0},{3,1},{4,2},{5,3},{6,4},{7,5},{10,8},{11,9},{12,10},{13,11},... | collective-permute-start | bytes 9437192 | tf_op jit(solution)/shard_map/ppermute | solution.py:17
  76.4 70.2 %collective-permute-start.3 = (f32[2,512]{1,0:T(2,128)S(1)}, f32[2,512]{1,0:T(2,128)S(1)}, u32[]{:S(2)}, u32[]{:S(2)}) collective-permute-start(f32[2,512]{1,0:T(2,128)S(1)} %fusion.83), channel_id=1, source_target_pairs={{2,0},{3,1},{4,2},{5,3},{6,4},{7,5},{10,8},{11,9},{12,10},{13,11},... | collective-permute-start | bytes 12296 | tf_op jit(solution)/shard_map/ppermute | solution.py:17
  78.4 68.3 %collective-permute-start.1 = (f32[2,1024]{1,0:T(2,128)S(1)}, f32[2,1024]{1,0:T(2,128)S(1)}, u32[]{:S(2)}, u32[]{:S(2)}) collective-permute-start(f32[2,1024]{1,0:T(2,128)S(1)} %pad_maximum_fusion.1), channel_id=1, source_target_pairs={{1,0},{2,1},{3,2},{4,3},{5,4},{6,5},{7,6},{9,8},{10,9},{11,10},{12... | collective-permute-start | bytes 24584 | tf_op jit(solution)/shard_map/ppermute | solution.py:17
  80.5 11.1 %copy-start = (f32[1536,1024]{1,0:T(8,128)S(1)}, f32[1536,1024]{1,0:T(8,128)}, u32[]{:S(2)}) copy-start(f32[1536,1024]{1,0:T(8,128)} %get-tuple-element.6) | copy-start | bytes 18874372
  91.6 2.8 copy-start.1
Sparse Core Ops, SparseCore 0:
  169.7 233.0 reduce-scatter.1

commit v3 on v2

--- a/solution.py
+++ b/solution.py
@@ -15,6 +15,34 @@
     count = lax.axis_size(axis)
     first, last = (max(0, -steps), min(count, count - steps))
     return lax.ppermute(value, axis, [(source, source + steps) for source in range(first, last)])
+
+
+def ring_steps(chunks, axis, count):
+    me = lax.axis_index(axis)
+    half = chunks.shape[-1] // 2
+    forward = [(i, (i + 1) % count) for i in range(count)]
+    backward = [(i, (i - 1) % count) for i in range(count)]
+
+    def own(index, part):
+        piece = lax.dynamic_index_in_dim(chunks, index % count, 0, keepdims=False)
+        return piece[..., :half] if part == 0 else piece[..., half:]
+
+    up = own(me - 1 + count, 0)
+    down = own(me + 1, 1)
+    for step in range(count - 1):
+        up = lax.ppermute(up, axis, forward) + own(me - step - 2 + 2 * count, 0)
+        down = lax.ppermute(down, axis, backward) + own(me + step + 2, 1)
+    return jnp.concatenate([up, down], axis=-1)
+
+
+def ring_reduce_scatter(value, major, minor):
+    major_count = lax.axis_size(major)
+    minor_count = lax.axis_size(minor)
+    rows = value.shape[0] // (major_count * minor_count)
+    grouped = value.reshape((major_count, minor_count, rows) + value.shape[1:])
+    by_minor = jnp.moveaxis(grouped, 1, 0)
+    partial = ring_steps(by_minor, minor, minor_count)
+    return ring_steps(partial, major, major_count)
 
 
 def samp_size():
@@ -79,12 +107,7 @@
         band_list = [tile(local_block, band_index) for band_index in range(band_limit)]
         row_list.append(jnp.stack(band_list, axis=1))
     tile_term = jnp.stack(row_list, axis=1)
-    reduced = lax.psum_scatter(
-        jnp.where(live_mask[None, :, :, None], tile_term, 0.0),
-        ("samp_x", "samp_z"),
-        scatter_dimension=0,
-        tiled=True,
-    )
+    reduced = ring_reduce_scatter(jnp.where(live_mask[None, :, :, None], tile_term, 0.0), "samp_x", "samp_z")
 
     own_rows = block_width // samp_size()
     row_start = (lax.axis_index("samp_x") * lax.axis_size("samp_z") + lax.axis_index("samp_z")) * own_rows

time: 412 us -> 397 us (0.964)
  waiting for transfers between devices: 285 us -> 222 us
  starting transfers between devices: 9.35 us -> 48.1 us
  between operations: 13.6 us -> 1.01 us
  local copies, waits for them, and re-layouts: 4.86 us -> 16.4 us
  other arithmetic: 19.7 us -> 25 us
    reduce_scatter x1 -> x0, waiting for transfers between devices: 233 us -> none  [on_device(): lax.psum_scatter(jnp.where(live_mask[None, :, :, None], tile_term, 0.0),...]
    ppermute x0 -> x20, waiting for transfers between devices: none -> 170 us  [the longest x10 109 us: ring_steps(): up = lax.ppermute(up, axis, forward) + own(me - step - 2 + 2 * count, 0)]
    ppermute x0 -> x20, starting transfers between devices: none -> 38.8 us  [the longest x10 38 us: ring_steps(): down = lax.ppermute(down, axis, backward) + own(me + step + 2, 1)]
    squeeze x0 -> x1, local copies, waits for them, and re-layouts: none -> 10.3 us  [own(): piece = lax.dynamic_index_in_dim(chunks, index % count, 0, keepdims=False)]
    add x0 -> x17, other arithmetic: none -> 6.35 us  [the longest x8 5.72 us: ring_steps(): down = lax.ppermute(down, axis, backward) + own(me + step + 2, 1)]
  transfers between devices with their start and end apart: 5 -> 24, of which waited for: 2 -> 19; matrix products, arithmetic and copies ran while one was open for 7% -> 8% of each run, Pallas kernels for 0% -> 0%
where the time goes in v3:
time: 397 us; the launch traced here: 394 us
  waiting for transfers between devices  222 us (56%)
  blocking collectives  50.9 us (13%)
  starting transfers between devices  48.1 us (12%)
  matrix products  30.5 us (8%)
  other arithmetic  25 us (6%)
  local copies, waits for them, and re-layouts  16.4 us (4%)
    ppermute x10, waiting for transfers between devices, ring_steps(): up = lax.ppermute(up, axis, forward) + own(me - step - 2 + 2 * count, 0)  109 us
    ppermute x10, waiting for transfers between devices, ring_steps(): down = lax.ppermute(down, axis, backward) + own(me + step + 2, 1)  60.9 us
    ppermute x4, waiting for transfers between devices, shifted(): lax.ppermute(value, axis, [(source, source + steps) for source in range(f...  52.1 us
    psum x4, blocking collectives, samp_sum(): return lax.psum(lax.psum(value, 'samp_z'), 'samp_x')  50.9 us
    ppermute x10, starting transfers between devices, ring_steps(): down = lax.ppermute(down, axis, backward) + own(me + step + 2, 1)  38 us
    dot_general x8, matrix products, tile(): lax.dot_general(left_panel, right_panel, transposed_dims, precision=HIGHE...  30.5 us
    squeeze x1, local copies, waits for them, and re-layouts, own(): piece = lax.dynamic_index_in_dim(chunks, index % count, 0, keepdims=False)  10.3 us
    ppermute x4, starting transfers between devices, shifted(): lax.ppermute(value, axis, [(source, source + steps) for source in range(f...  9.34 us
  transfers between devices with their start and end apart: 24, of which 19 were waited for; matrix products, arithmetic and copies ran while one was open for 8% of the time, Pallas kernels for 0%

profile of v3, /device:TPU:8, one launch (start us, length us, event | category | flops | bytes accessed | tf_op | source)
XLA Modules:
  0.0 394.3 jit_solution(12927820795404899224)
XLA Ops:
  1.9 3.8 slice.165
  5.8 3.4 collective-permute-start.2
  9.2 3.2 reduce_sum.18
  12.4 18.5 %psum.28 = f32[1024]{0:T(1024)S(1)} all-reduce(f32[1024]{0:T(1024)S(1)} %reduce_sum.18), channel_id=1, replica_groups=mesh['samp_x'=4,'samp_z'=8,'snp'=8] {'samp_z'}, use_global_device_ids=true, to_apply=%region_1.0 | all-reduce | flops 1024 | bytes 8192 | tf_op jit(solution)/shard_map/psum | solution.py:53
  30.9 10.5 %psum.29 = f32[1024]{0:T(1024)S(1)} all-reduce(f32[1024]{0:T(1024)S(1)} %psum.28), channel_id=1, replica_groups=mesh['samp_x'=4,'samp_z'=8,'snp'=8] {'samp_x'}, use_global_device_ids=true, to_apply=%region_2.0 | all-reduce | flops 1024 | bytes 8192 | tf_op jit(solution)/shard_map/psum | solution.py:53
  41.4 6.6 %multiply_reduce_fusion = (f32[1024]{0:T(1024)S(1)}, f32[1536,1024]{1,0:T(8,128)}) fusion(f32[1536,1024]{1,0:T(8,128)} %param.2, f32[1024]{0:T(1024)S(1)} %broadcast_multiply_fusion), kind=kLoop, calls=%fused_computation.1 | loop fusion | flops 4717568 | bytes 12591104 | tf_op jit(solution)/shard_map/reduce_sum | solution.py:76
  48.0 14.1 %psum.30 = f32[1024]{0:T(1024)S(1)} all-reduce(f32[1024]{0:T(1024)S(1)} %get-tuple-element.5), channel_id=1, replica_groups=mesh['samp_x'=4,'samp_z'=8,'snp'=8] {'samp_z'}, use_global_device_ids=true, to_apply=%region_4.0 | all-reduce | flops 1024 | bytes 8192 | tf_op jit(solution)/shard_map/psum | solution.py:53
  62.1 7.7 %psum.31 = f32[1024]{0:T(1024)S(1)} all-reduce(f32[1024]{0:T(1024)S(1)} %psum.30), channel_id=1, replica_groups=mesh['samp_x'=4,'samp_z'=8,'snp'=8] {'samp_x'}, use_global_device_ids=true, to_apply=%region_5.0 | all-reduce | flops 1024 | bytes 8192 | tf_op jit(solution)/shard_map/psum | solution.py:53
  74.1 5.6 %fusion.14 = f32[512,512]{1,0:T(8,128)S(1)} fusion(f32[1536,1024]{1,0:T(8,128)} %get-tuple-element.6), kind=kOutput, calls=%fused_computation.18 | convolution fusion | flops 2415919104 | bytes 4194304 | tf_op jit(solution)/shard_map/dot_general | solution.py:95
  79.8 5.5 %fusion.19 = f32[512,512]{1,0:T(8,128)S(1)} fusion(f32[1536,1024]{1,0:T(8,128)} %get-tuple-element.6), kind=kOutput, calls=%fused_computation.23 | convolution fusion | flops 2415919104 | bytes 4194304 | tf_op jit(solution)/shard_map/dot_general | solution.py:95
  85.3 2.8 fusion.12
  88.2 52.1 %collective-permute-done.3 = f32[2,512]{1,0:T(2,128)S(1)} collective-permute-done((f32[2,512]{1,0:T(2,128)S(1)}, f32[2,512]{1,0:T(2,128)S(1)}, u32[]{:S(2)}, u32[]{:S(2)}) %collective-permute-start.3) | collective-permute-done | bytes 4128 | tf_op jit(solution)/shard_map/ppermute | solution.py:17
  140.3 5.6 %fusion = f32[512,512]{1,0:T(8,128)S(1)} fusion(f32[1536,512]{1,0:T(8,128)} %collective-permute-done.2, f32[1536,1024]{1,0:T(8,128)} %get-tuple-element.6, f32[512]{0:T(512)S(1)} %bitcast.157), kind=kOutput, calls=%fused_computation.2 | convolution fusion | flops 2416705536 | bytes 7342080 | tf_op jit(solution)/shard_map/dot_general | solution.py:95
  145.9 3.9 broadcast_subtract_fusion
  149.8 2.7 fusion.4
  152.6 2.7 fusion.6
  155.3 2.7 fusion.2
  158.1 2.7 fusion.8
  160.9 4.5 %maximum_select_fusion = f32[4,8,16,2,4,512]{5,2,4,3,1,0:T(8,128)} fusion(f32[4,8,16,1,1,512]{5,2,4,3,1,0:T(8,128)S(1)} %bitcast.146, f32[4,8,16,1,1,512]{5,2,4,3,1,0:T(8,128)S(1)} %bitcast.144, f32[4,8,16,1,1,512]{5,2,4,3,1,0:T(8,128)S(1)} %bitcast.143, f32[4,8,16,1,1,512]{5,2,4,3,1,0:T(8,128)S(1)} %bitcast.148, f32[4,8,16,1,1,512]{5,2,4,3,1,0:T(8,128)S(1)} %bitcast.142, ...), kind=kLoop, calls=%fused_computation | loop fusion | flops 16777216 | bytes 16777224 | tf_op jit(solution)/shard_map/jit(_where)/select_n | solution.py:110
  165.3 10.3 %dynamic-slice_bitcast_fusion = (f32[4,16,2,4,512]{4,1,3,2,0:T(8,128)}, f32[4,16,2,4,512]{4,1,3,2,0:T(8,128)}, f32[4,16,2,4,512]{4,1,3,2,0:T(8,128)}, f32[4,16,2...) fusion(f32[4,8,16,2,4,512]{5,2,4,3,1,0:T(8,128)} %maximum_selec, ...), kind=kLoop, calls=%fused_computation.39 | loop fusion | bytes 29360184 | tf_op jit(solution)/shard_map/jit(dynamic_index_in_dim)/squeeze | solution.py:27
  176.9 5.9 %collective-permute-start.11 = (f32[4,16,2,4,256]{4,1,3,2,0:T(8,128)S(1)}, f32[4,16,2,4,256]{4,1,3,2,0:T(8,128)S(1)}, u32[]{:S(2)}, u32[]{:S(2)}) collective-permute-start(f32[4,16,2,4,256]{4,1,3,2,0:T(8,128)S(1)} %slice.224), channel_id=1, source_target_pairs={{0,56},{8,0},{16,8},{24,16},{32,24},{40,32},{48,40},{56,48},{1,57}... | collective-permute-start | bytes 1572872 | tf_op jit(solution)/shard_map/ppermute | solution.py:34
  182.8 11.4 %collective-permute-done.11 = f32[4,16,2,4,256]{4,1,3,2,0:T(8,128)S(1)} collective-permute-done((f32[4,16,2,4,256]{4,1,3,2,0:T(8,128)S(1)}, f32[4,16,2,4,256]{4,1,3,2,0:T(8,128)S(1)}, u32[]{:S(2)}, u32[]{:S(2)}) %collective-permute-start.11) | collective-permute-done | bytes 524320 | tf_op jit(solution)/shard_map/ppermute | solution.py:34
  195.3 3.8 collective-permute-start.12
  199.1 10.6 %collective-permute-done.12 = f32[4,16,2,4,256]{4,1,3,2,0:T(8,128)S(1)} collective-permute-done((f32[4,16,2,4,256]{4,1,3,2,0:T(8,128)S(1)}, f32[4,16,2,4,256]{4,1,3,2,0:T(8,128)S(1)}, u32[]{:S(2)}, u32[]{:S(2)}) %collective-permute-start.12) | collective-permute-done | bytes 524320 | tf_op jit(solution)/shard_map/ppermute | solution.py:34
  210.8 3.8 collective-permute-start.13
  214.6 9.7 %collective-permute-done.13 = f32[4,16,2,4,256]{4,1,3,2,0:T(8,128)S(1)} collective-permute-done((f32[4,16,2,4,256]{4,1,3,2,0:T(8,128)S(1)}, f32[4,16,2,4,256]{4,1,3,2,0:T(8,128)S(1)}, u32[]{:S(2)}, u32[]{:S(2)}) %collective-permute-start.13) | collective-permute-done | bytes 524320 | tf_op jit(solution)/shard_map/ppermute | solution.py:34
  225.4 3.8 collective-permute-start.14
  229.2 8.8 %collective-permute-done.14 = f32[4,16,2,4,256]{4,1,3,2,0:T(8,128)S(1)} collective-permute-done((f32[4,16,2,4,256]{4,1,3,2,0:T(8,128)S(1)}, f32[4,16,2,4,256]{4,1,3,2,0:T(8,128)S(1)}, u32[]{:S(2)}, u32[]{:S(2)}) %collective-permute-start.14) | collective-permute-done | bytes 524320 | tf_op jit(solution)/shard_map/ppermute | solution.py:34
  239.2 3.8 collective-permute-start.15
  242.9 8.2 %collective-permute-done.15 = f32[4,16,2,4,256]{4,1,3,2,0:T(8,128)S(1)} collective-permute-done((f32[4,16,2,4,256]{4,1,3,2,0:T(8,128)S(1)}, f32[4,16,2,4,256]{4,1,3,2,0:T(8,128)S(1)}, u32[]{:S(2)}, u32[]{:S(2)}) %collective-permute-start.15) | collective-permute-done | bytes 524320 | tf_op jit(solution)/shard_map/ppermute | solution.py:34
  251.2 3.8 collective-permute-start.16
  255.0 7.1 %collective-permute-done.16 = f32[4,16,2,4,256]{4,1,3,2,0:T(8,128)S(1)} collective-permute-done((f32[4,16,2,4,256]{4,1,3,2,0:T(8,128)S(1)}, f32[4,16,2,4,256]{4,1,3,2,0:T(8,128)S(1)}, u32[]{:S(2)}, u32[]{:S(2)}) %collective-permute-start.16) | collective-permute-done | bytes 524320 | tf_op jit(solution)/shard_map/ppermute | solution.py:34
  263.1 12.8 %collective-permute-done.4 = f32[4,16,2,4,256]{4,1,3,2,0:T(8,128)S(1)} collective-permute-done((f32[4,16,2,4,256]{4,1,3,2,0:T(8,128)S(1)}, f32[4,16,2,4,256]{4,1,3,2,0:T(8,128)S(1)}, u32[]{:S(2)}, u32[]{:S(2)}) %collective-permute-start.4) | collective-permute-done | bytes 524320 | tf_op jit(solution)/shard_map/ppermute | solution.py:33
  276.1 14.0 %collective-permute-done.5 = f32[4,16,2,4,256]{4,1,3,2,0:T(8,128)S(1)} collective-permute-done((f32[4,16,2,4,256]{4,1,3,2,0:T(8,128)S(1)}, f32[4,16,2,4,256]{4,1,3,2,0:T(8,128)S(1)}, u32[]{:S(2)}, u32[]{:S(2)}) %collective-permute-start.5) | collective-permute-done | bytes 524320 | tf_op jit(solution)/shard_map/ppermute | solution.py:33
  290.3 14.9 %collective-permute-done.6 = f32[4,16,2,4,256]{4,1,3,2,0:T(8,128)S(1)} collective-permute-done((f32[4,16,2,4,256]{4,1,3,2,0:T(8,128)S(1)}, f32[4,16,2,4,256]{4,1,3,2,0:T(8,128)S(1)}, u32[]{:S(2)}, u32[]{:S(2)}) %collective-permute-start.6) | collective-permute-done | bytes 524320 | tf_op jit(solution)/shard_map/ppermute | solution.py:33
  305.4 15.9 %collective-permute-done.7 = f32[4,16,2,4,256]{4,1,3,2,0:T(8,128)S(1)} collective-permute-done((f32[4,16,2,4,256]{4,1,3,2,0:T(8,128)S(1)}, f32[4,16,2,4,256]{4,1,3,2,0:T(8,128)S(1)}, u32[]{:S(2)}, u32[]{:S(2)}) %collective-permute-start.7) | collective-permute-done | bytes 524320 | tf_op jit(solution)/shard_map/ppermute | solution.py:33
  321.6 15.1 %collective-permute-done.8 = f32[4,16,2,4,256]{4,1,3,2,0:T(8,128)S(1)} collective-permute-done((f32[4,16,2,4,256]{4,1,3,2,0:T(8,128)S(1)}, f32[4,16,2,4,256]{4,1,3,2,0:T(8,128)S(1)}, u32[]{:S(2)}, u32[]{:S(2)}) %collective-permute-start.8) | collective-permute-done | bytes 524320 | tf_op jit(solution)/shard_map/ppermute | solution.py:33
  336.8 3.4 collective-permute-start.17
  340.3 10.8 %collective-permute-done.9 = f32[4,16,2,4,256]{4,1,3,2,0:T(8,128)S(1)} collective-permute-done((f32[4,16,2,4,256]{4,1,3,2,0:T(8,128)S(1)}, f32[4,16,2,4,256]{4,1,3,2,0:T(8,128)S(1)}, u32[]{:S(2)}, u32[]{:S(2)}) %collective-permute-start.9) | collective-permute-done | bytes 524320 | tf_op jit(solution)/shard_map/ppermute | solution.py:33
  351.3 10.3 %collective-permute-done.10 = f32[4,16,2,4,256]{4,1,3,2,0:T(8,128)S(1)} collective-permute-done((f32[4,16,2,4,256]{4,1,3,2,0:T(8,128)S(1)}, f32[4,16,2,4,256]{4,1,3,2,0:T(8,128)S(1)}, u32[]{:S(2)}, u32[]{:S(2)}) %collective-permute-start.10) | collective-permute-done | bytes 524320 | tf_op jit(solution)/shard_map/ppermute | solution.py:33
  362.0 2.9 collective-permute-start.21
  364.9 2.5 collective-permute-done.21
  367.4 3.7 collective-permute-start.22
  371.1 2.5 collective-permute-done.22
  373.8 6.6 %collective-permute-done.18 = f32[16,2,4,256]{3,0,2,1:T(8,128)S(1)} collective-permute-done((f32[16,2,4,256]{3,0,2,1:T(8,128)S(1)}, f32[16,2,4,256]{3,0,2,1:T(8,128)S(1)}, u32[]{:S(2)}, u32[]{:S(2)}) %collective-permute-start.18) | collective-permute-done | bytes 131104 | tf_op jit(solution)/shard_map/ppermute | solution.py:33
  380.6 3.2 collective-permute-start.23
  383.8 2.8 collective-permute-done.19
  386.8 6.1 %collective-permute-done.20 = f32[16,2,4,256]{3,0,2,1:T(8,128)S(1)} collective-permute-done((f32[16,2,4,256]{3,0,2,1:T(8,128)S(1)}, f32[16,2,4,256]{3,0,2,1:T(8,128)S(1)}, u32[]{:S(2)}, u32[]{:S(2)}) %collective-permute-start.20) | collective-permute-done | bytes 131104 | tf_op jit(solution)/shard_map/ppermute | solution.py:33
  (75 shorter events, 15.8 us)
Async XLA Ops:
  0.0 145.9 %collective-permute-start = (f32[1536,1024]{1,0:T(8,128)}, f32[1536,1024]{1,0:T(8,128)}, u32[]{:S(2)}, u32[]{:S(2)}) collective-permute-start(f32[1536,1024]{1,0:T(8,128)} %param.2), channel_id=1, source_target_pairs={{1,0},{2,1},{3,2},{4,3},{5,4},{6,5},{7,6},{9,8},{10,9},{11,10},{12... | collective-permute-start | bytes 18874376 | tf_op jit(solution)/shard_map/ppermute | solution.py:17
  5.8 134.5 %collective-permute-start.2 = (f32[1536,512]{1,0:T(8,128)}, f32[1536,512]{1,0:T(8,128)}, u32[]{:S(2)}, u32[]{:S(2)}) collective-permute-start(f32[1536,512]{1,0:T(8,128)} %slice.165), channel_id=1, source_target_pairs={{2,0},{3,1},{4,2},{5,3},{6,4},{7,5},{10,8},{11,9},{12,10},{13,11},... | collective-permute-start | bytes 9437192 | tf_op jit(solution)/shard_map/ppermute | solution.py:17
  41.4 32.7 %copy-start.7 = (s32[2]{0:T(128)S(1)}, s32[2]{0:T(128)}, u32[]{:S(2)}) copy-start(s32[2]{0:T(128)} %param.3) | copy-start | bytes 28
  69.9 70.4 %collective-permute-start.1 = (f32[2,1024]{1,0:T(2,128)S(1)}, f32[2,1024]{1,0:T(2,128)S(1)}, u32[]{:S(2)}, u32[]{:S(2)}) collective-permute-start(f32[2,1024]{1,0:T(2,128)S(1)} %pad_maximum_fusion.2), channel_id=1, source_target_pairs={{1,0},{2,1},{3,2},{4,3},{5,4},{6,5},{7,6},{9,8},{10,9},{11,10},{12... | collective-permute-start | bytes 24584 | tf_op jit(solution)/shard_map/ppermute | solution.py:17
  71.8 68.4 %collective-permute-start.3 = (f32[2,512]{1,0:T(2,128)S(1)}, f32[2,512]{1,0:T(2,128)S(1)}, u32[]{:S(2)}, u32[]{:S(2)}) collective-permute-start(f32[2,512]{1,0:T(2,128)S(1)} %fusion.74), channel_id=1, source_target_pairs={{2,0},{3,1},{4,2},{5,3},{6,4},{7,5},{10,8},{11,9},{12,10},{13,11},... | collective-permute-start | bytes 12296 | tf_op jit(solution)/shard_map/ppermute | solution.py:17
  74.1 11.2 %copy-start = (f32[1536,1024]{1,0:T(8,128)S(1)}, f32[1536,1024]{1,0:T(8,128)}, u32[]{:S(2)}) copy-start(f32[1536,1024]{1,0:T(8,128)} %get-tuple-element.6) | copy-start | bytes 18874372
  140.3 9.6 %slice-start = ((s8[6291456]{0:T(1024)(128)(4,1)}), s8[4194304]{0:T(1024)(128)(4,1)S(1)}, s32[]{:S(2)}) async-start(s8[6291456]{0:T(1024)(128)(4,1)} %bitcast.139), calls=%async_computation | async-start | bytes 8388608
  145.9 3.9 slice-start.1
  175.6 75.6 %copy-start.6 = (f32[4,16,2,4,512]{4,1,3,2,0:T(8,128)S(1)}, f32[4,16,2,4,512]{4,1,3,2,0:T(8,128)}, u32[]{:S(2)}) copy-start(f32[4,16,2,4,512]{4,1,3,2,0:T(8,128)} %get-tuple-element.7) | copy-start | bytes 3145732
  175.6 100.3 %copy-start.5 = (f32[4,16,2,4,512]{4,1,3,2,0:T(8,128)S(1)}, f32[4,16,2,4,512]{4,1,3,2,0:T(8,128)}, u32[]{:S(2)}) copy-start(f32[4,16,2,4,512]{4,1,3,2,0:T(8,128)} %get-tuple-element.19) | copy-start | bytes 3145732
  176.8 113.3 %copy-start.4 = (f32[4,16,2,4,512]{4,1,3,2,0:T(8,128)S(1)}, f32[4,16,2,4,512]{4,1,3,2,0:T(8,128)}, u32[]{:S(2)}) copy-start(f32[4,16,2,4,512]{4,1,3,2,0:T(8,128)} %get-tuple-element.18) | copy-start | bytes 3145732
  176.9 17.3 %collective-permute-start.11 = (f32[4,16,2,4,256]{4,1,3,2,0:T(8,128)S(1)}, f32[4,16,2,4,256]{4,1,3,2,0:T(8,128)S(1)}, u32[]{:S(2)}, u32[]{:S(2)}) collective-permute-start(f32[4,16,2,4,256]{4,1,3,2,0:T(8,128)S(1)} %slice.224), channel_id=1, source_target_pairs={{0,56},{8,0},{16,8},{24,16},{32,24},{40,32},{48,40},{56,48},{1,57}... | collective-permute-start | bytes 1572872 | tf_op jit(solution)/shard_map/ppermute | solution.py:34
  195.3 109.9 %copy-start.3 = (f32[4,16,2,4,512]{4,1,3,2,0:T(8,128)S(1)}, f32[4,16,2,4,512]{4,1,3,2,0:T(8,128)}, u32[]{:S(2)}) copy-start(f32[4,16,2,4,512]{4,1,3,2,0:T(8,128)} %get-tuple-element.17) | copy-start | bytes 3145732
  195.3 14.3 %collective-permute-start.12 = (f32[4,16,2,4,256]{4,1,3,2,0:T(8,128)S(1)}, f32[4,16,2,4,256]{4,1,3,2,0:T(8,128)S(1)}, u32[]{:S(2)}, u32[]{:S(2)}) collective-permute-start(f32[4,16,2,4,256]{4,1,3,2,0:T(8,128)S(1)} %slice_add_fusion.6), channel_id=1, source_target_pairs={{0,56},{8,0},{16,8},{24,16},{32,24},{40,32},{48,40},{56,48},{1,57}... | collective-permute-start | bytes 1572872 | tf_op jit(solution)/shard_map/ppermute | solution.py:34
  210.8 110.6 %copy-start.2 = (f32[4,16,2,4,512]{4,1,3,2,0:T(8,128)S(1)}, f32[4,16,2,4,512]{4,1,3,2,0:T(8,128)}, u32[]{:S(2)}) copy-start(f32[4,16,2,4,512]{4,1,3,2,0:T(8,128)} %get-tuple-element.16) | copy-start | bytes 3145732
  210.8 13.5 %collective-permute-start.13 = (f32[4,16,2,4,256]{4,1,3,2,0:T(8,128)S(1)}, f32[4,16,2,4,256]{4,1,3,2,0:T(8,128)S(1)}, u32[]{:S(2)}, u32[]{:S(2)}) collective-permute-start(f32[4,16,2,4,256]{4,1,3,2,0:T(8,128)S(1)} %slice_add_fusion.5), channel_id=1, source_target_pairs={{0,56},{8,0},{16,8},{24,16},{32,24},{40,32},{48,40},{56,48},{1,57}... | collective-permute-start | bytes 1572872 | tf_op jit(solution)/shard_map/ppermute | solution.py:34
  225.4 111.2 %copy-start.1 = (f32[4,16,2,4,512]{4,1,3,2,0:T(8,128)S(1)}, f32[4,16,2,4,512]{4,1,3,2,0:T(8,128)}, u32[]{:S(2)}) copy-start(f32[4,16,2,4,512]{4,1,3,2,0:T(8,128)} %get-tuple-element.15) | copy-start | bytes 3145732
  225.4 12.6 %collective-permute-start.14 = (f32[4,16,2,4,256]{4,1,3,2,0:T(8,128)S(1)}, f32[4,16,2,4,256]{4,1,3,2,0:T(8,128)S(1)}, u32[]{:S(2)}, u32[]{:S(2)}) collective-permute-start(f32[4,16,2,4,256]{4,1,3,2,0:T(8,128)S(1)} %slice_add_fusion.4), channel_id=1, source_target_pairs={{0,56},{8,0},{16,8},{24,16},{32,24},{40,32},{48,40},{56,48},{1,57}... | collective-permute-start | bytes 1572872 | tf_op jit(solution)/shard_map/ppermute | solution.py:34
  239.2 12.0 %collective-permute-start.15 = (f32[4,16,2,4,256]{4,1,3,2,0:T(8,128)S(1)}, f32[4,16,2,4,256]{4,1,3,2,0:T(8,128)S(1)}, u32[]{:S(2)}, u32[]{:S(2)}) collective-permute-start(f32[4,16,2,4,256]{4,1,3,2,0:T(8,128)S(1)} %slice_add_fusion.3), channel_id=1, source_target_pairs={{0,56},{8,0},{16,8},{24,16},{32,24},{40,32},{48,40},{56,48},{1,57}... | collective-permute-start | bytes 1572872 | tf_op jit(solution)/shard_map/ppermute | solution.py:34
  251.2 10.9 %collective-permute-start.16 = (f32[4,16,2,4,256]{4,1,3,2,0:T(8,128)S(1)}, f32[4,16,2,4,256]{4,1,3,2,0:T(8,128)S(1)}, u32[]{:S(2)}, u32[]{:S(2)}) collective-permute-start(f32[4,16,2,4,256]{4,1,3,2,0:T(8,128)S(1)} %slice_add_fusion.2), channel_id=1, source_target_pairs={{0,56},{8,0},{16,8},{24,16},{32,24},{40,32},{48,40},{56,48},{1,57}... | collective-permute-start | bytes 1572872 | tf_op jit(solution)/shard_map/ppermute | solution.py:34
  263.1 12.8 %collective-permute-start.4 = (f32[4,16,2,4,256]{4,1,3,2,0:T(8,128)S(1)}, f32[4,16,2,4,256]{4,1,3,2,0:T(8,128)S(1)}, u32[]{:S(2)}, u32[]{:S(2)}) collective-permute-start(f32[4,16,2,4,256]{4,1,3,2,0:T(8,128)S(1)} %get-tuple-element.30), channel_id=1, source_target_pairs={{0,8},{8,16},{16,24},{24,32},{32,40},{40,48},{48,56},{56,0},{1,9},... | collective-permute-start | bytes 1572872 | tf_op jit(solution)/shard_map/ppermute | solution.py:33
  276.0 14.1 %collective-permute-start.5 = (f32[4,16,2,4,256]{4,1,3,2,0:T(8,128)S(1)}, f32[4,16,2,4,256]{4,1,3,2,0:T(8,128)S(1)}, u32[]{:S(2)}, u32[]{:S(2)}) collective-permute-start(f32[4,16,2,4,256]{4,1,3,2,0:T(8,128)S(1)} %slice_add_fusion.13), channel_id=1, source_target_pairs={{0,8},{8,16},{16,24},{24,32},{32,40},{40,48},{48,56},{56,0},{1,9},... | collective-permute-start | bytes 1572872 | tf_op jit(solution)/shard_map/ppermute | solution.py:33
  290.3 15.0 %collective-permute-start.6 = (f32[4,16,2,4,256]{4,1,3,2,0:T(8,128)S(1)}, f32[4,16,2,4,256]{4,1,3,2,0:T(8,128)S(1)}, u32[]{:S(2)}, u32[]{:S(2)}) collective-permute-start(f32[4,16,2,4,256]{4,1,3,2,0:T(8,128)S(1)} %slice_add_fusion.12), channel_id=1, source_target_pairs={{0,8},{8,16},{16,24},{24,32},{32,40},{40,48},{48,56},{56,0},{1,9},... | collective-permute-start | bytes 1572872 | tf_op jit(solution)/shard_map/ppermute | solution.py:33
  305.4 16.0 %collective-permute-start.7 = (f32[4,16,2,4,256]{4,1,3,2,0:T(8,128)S(1)}, f32[4,16,2,4,256]{4,1,3,2,0:T(8,128)S(1)}, u32[]{:S(2)}, u32[]{:S(2)}) collective-permute-start(f32[4,16,2,4,256]{4,1,3,2,0:T(8,128)S(1)} %slice_add_fusion.11), channel_id=1, source_target_pairs={{0,8},{8,16},{16,24},{24,32},{32,40},{40,48},{48,56},{56,0},{1,9},... | collective-permute-start | bytes 1572872 | tf_op jit(solution)/shard_map/ppermute | solution.py:33
  321.5 15.2 %collective-permute-start.8 = (f32[4,16,2,4,256]{4,1,3,2,0:T(8,128)S(1)}, f32[4,16,2,4,256]{4,1,3,2,0:T(8,128)S(1)}, u32[]{:S(2)}, u32[]{:S(2)}) collective-permute-start(f32[4,16,2,4,256]{4,1,3,2,0:T(8,128)S(1)} %slice_add_fusion.10), channel_id=1, source_target_pairs={{0,8},{8,16},{16,24},{24,32},{32,40},{40,48},{48,56},{56,0},{1,9},... | collective-permute-start | bytes 1572872 | tf_op jit(solution)/shard_map/ppermute | solution.py:33
  336.7 14.3 %collective-permute-start.9 = (f32[4,16,2,4,256]{4,1,3,2,0:T(8,128)S(1)}, f32[4,16,2,4,256]{4,1,3,2,0:T(8,128)S(1)}, u32[]{:S(2)}, u32[]{:S(2)}) collective-permute-start(f32[4,16,2,4,256]{4,1,3,2,0:T(8,128)S(1)} %slice_add_fusion.9), channel_id=1, source_target_pairs={{0,8},{8,16},{16,24},{24,32},{32,40},{40,48},{48,56},{56,0},{1,9},... | collective-permute-start | bytes 1572872 | tf_op jit(solution)/shard_map/ppermute | solution.py:33
  336.8 14.5 %collective-permute-start.17 = (f32[4,16,2,4,256]{4,1,3,2,0:T(8,128)}, f32[4,16,2,4,256]{4,1,3,2,0:T(8,128)S(1)}, u32[]{:S(2)}, u32[]{:S(2)}) collective-permute-start(f32[4,16,2,4,256]{4,1,3,2,0:T(8,128)} %get-tuple-element.29), channel_id=1, source_target_pairs={{0,56},{8,0},{16,8},{24,16},{32,24},{40,32},{48,40},{56,48},{1,57}... | collective-permute-start | bytes 1572872 | tf_op jit(solution)/shard_map/ppermute | solution.py:34
  351.1 10.5 %collective-permute-start.10 = (f32[4,16,2,4,256]{4,1,3,2,0:T(8,128)S(1)}, f32[4,16,2,4,256]{4,1,3,2,0:T(8,128)S(1)}, u32[]{:S(2)}, u32[]{:S(2)}) collective-permute-start(f32[4,16,2,4,256]{4,1,3,2,0:T(8,128)S(1)} %slice_add_fusion.8), channel_id=1, source_target_pairs={{0,8},{8,16},{16,24},{24,32},{32,40},{40,48},{48,56},{56,0},{1,9},... | collective-permute-start | bytes 1572872 | tf_op jit(solution)/shard_map/ppermute | solution.py:33
  362.0 5.4 %collective-permute-start.21 = (f32[16,2,4,256]{3,0,2,1:T(8,128)S(1)}, f32[16,2,4,256]{3,0,2,1:T(8,128)S(1)}, u32[]{:S(2)}, u32[]{:S(2)}) collective-permute-start(f32[16,2,4,256]{3,0,2,1:T(8,128)S(1)} %slice.236), channel_id=1, source_target_pairs={{0,192},{64,0},{128,64},{192,128},{1,193},{65,1},{129,65},{193,129... | collective-permute-start | bytes 393224 | tf_op jit(solution)/shard_map/ppermute | solution.py:34
  367.4 6.3 %collective-permute-start.22 = (f32[16,2,4,256]{3,0,2,1:T(8,128)S(1)}, f32[16,2,4,256]{3,0,2,1:T(8,128)S(1)}, u32[]{:S(2)}, u32[]{:S(2)}) collective-permute-start(f32[16,2,4,256]{3,0,2,1:T(8,128)S(1)} %slice_add_fusion.16), channel_id=1, source_target_pairs={{0,192},{64,0},{128,64},{192,128},{1,193},{65,1},{129,65},{193,129... | collective-permute-start | bytes 393224 | tf_op jit(solution)/shard_map/ppermute | solution.py:34
  373.7 6.7 %collective-permute-start.18 = (f32[16,2,4,256]{3,0,2,1:T(8,128)S(1)}, f32[16,2,4,256]{3,0,2,1:T(8,128)S(1)}, u32[]{:S(2)}, u32[]{:S(2)}) collective-permute-start(f32[16,2,4,256]{3,0,2,1:T(8,128)S(1)} %get-tuple-element.45), channel_id=1, source_target_pairs={{0,64},{64,128},{128,192},{192,0},{1,65},{65,129},{129,193},{193,1... | collective-permute-start | bytes 393224 | tf_op jit(solution)/shard_map/ppermute | solution.py:33
  380.4 6.3 %collective-permute-start.19 = (f32[16,2,4,256]{3,0,2,1:T(8,128)S(1)}, f32[16,2,4,256]{3,0,2,1:T(8,128)S(1)}, u32[]{:S(2)}, u32[]{:S(2)}) collective-permute-start(f32[16,2,4,256]{3,0,2,1:T(8,128)S(1)} %slice_add_fusion.19), channel_id=1, source_target_pairs={{0,64},{64,128},{128,192},{192,0},{1,65},{65,129},{129,193},{193,1... | collective-permute-start | bytes 393224 | tf_op jit(solution)/shard_map/ppermute | solution.py:33
  380.6 6.2 %collective-permute-start.23 = (f32[16,2,4,256]{3,0,2,1:T(8,128)S(1)}, f32[16,2,4,256]{3,0,2,1:T(8,128)S(1)}, u32[]{:S(2)}, u32[]{:S(2)}) collective-permute-start(f32[16,2,4,256]{3,0,2,1:T(8,128)S(1)} %get-tuple-element.46), channel_id=1, source_target_pairs={{0,192},{64,0},{128,64},{192,128},{1,193},{65,1},{129,65},{193,129... | collective-permute-start | bytes 393224 | tf_op jit(solution)/shard_map/ppermute | solution.py:34
  386.7 6.3 %collective-permute-start.20 = (f32[16,2,4,256]{3,0,2,1:T(8,128)S(1)}, f32[16,2,4,256]{3,0,2,1:T(8,128)S(1)}, u32[]{:S(2)}, u32[]{:S(2)}) collective-permute-start(f32[16,2,4,256]{3,0,2,1:T(8,128)S(1)} %slice_add_fusion.18), channel_id=1, source_target_pairs={{0,64},{64,128},{128,192},{192,0},{1,65},{65,129},{129,193},{193,1... | collective-permute-start | bytes 393224 | tf_op jit(solution)/shard_map/ppermute | solution.py:33

commit v4 on v3

--- a/solution.py
+++ b/solution.py
@@ -30,6 +30,7 @@
     up = own(me - 1 + count, 0)
     down = own(me + 1, 1)
     for step in range(count - 1):
+        up, down = lax.optimization_barrier((up, down))
         up = lax.ppermute(up, axis, forward) + own(me - step - 2 + 2 * count, 0)
         down = lax.ppermute(down, axis, backward) + own(me + step + 2, 1)
     return jnp.concatenate([up, down], axis=-1)

time: 397 us -> 304 us (0.77)
  waiting for transfers between devices: 222 us -> 141 us
  starting transfers between devices: 48.1 us -> 37.5 us
    ppermute x10, waiting for transfers between devices: 109 us -> 25.1 us  [ring_steps(): up = lax.ppermute(up, axis, forward) + own(me - step - 2 + 2 * count, 0)]
    ppermute x10, starting transfers between devices: 38 us -> 17.8 us  [ring_steps(): down = lax.ppermute(down, axis, backward) + own(me + step + 2, 1)]
    ppermute x10, starting transfers between devices: 0.75 us -> 10.4 us  [ring_steps(): up = lax.ppermute(up, axis, forward) + own(me - step - 2 + 2 * count, 0)]
  transfers between devices with their start and end apart: 24 -> 24, of which waited for: 19 -> 20; matrix products, arithmetic and copies ran while one was open for 8% -> 12% of each run, Pallas kernels for 0% -> 0%
where the time goes in v4:
time: 304 us; the launch traced here: 301 us
  waiting for transfers between devices  141 us (46%)
  blocking collectives  50.9 us (17%)
  starting transfers between devices  37.5 us (12%)
  matrix products  30.5 us (10%)
  other arithmetic  24 us (8%)
  local copies, waits for them, and re-layouts  16.5 us (5%)
    ppermute x10, waiting for transfers between devices, ring_steps(): down = lax.ppermute(down, axis, backward) + own(me + step + 2, 1)  63.8 us
    ppermute x4, waiting for transfers between devices, shifted(): lax.ppermute(value, axis, [(source, source + steps) for source in range(f...  52.1 us
    psum x4, blocking collectives, samp_sum(): return lax.psum(lax.psum(value, 'samp_z'), 'samp_x')  50.9 us
    dot_general x8, matrix products, tile(): lax.dot_general(left_panel, right_panel, transposed_dims, precision=HIGHE...  30.5 us
    ppermute x10, waiting for transfers between devices, ring_steps(): up = lax.ppermute(up, axis, forward) + own(me - step - 2 + 2 * count, 0)  25.1 us
    ppermute x10, starting transfers between devices, ring_steps(): down = lax.ppermute(down, axis, backward) + own(me + step + 2, 1)  17.8 us
    ppermute x10, starting transfers between devices, ring_steps(): up = lax.ppermute(up, axis, forward) + own(me - step - 2 + 2 * count, 0)  10.4 us
    squeeze x1, local copies, waits for them, and re-layouts, own(): piece = lax.dynamic_index_in_dim(chunks, index % count, 0, keepdims=False)  10.3 us
  transfers between devices with their start and end apart: 24, of which 20 were waited for; matrix products, arithmetic and copies ran while one was open for 12% of the time, Pallas kernels for 0%

profile of v4, /device:TPU:8, one launch (start us, length us, event | category | flops | bytes accessed | tf_op | source)
XLA Modules:
  0.0 301.2 jit_solution(5572488978329821540)
XLA Ops:
  0.0 1.9 collective-permute-start
  1.9 3.9 %slice.165 = f32[1536,512]{1,0:T(8,128)} slice(f32[1536,1024]{1,0:T(8,128)} %param.2), slice={[0:1536], [0:512]} | slice | bytes 6291456 | tf_op jit(solution)/shard_map/slice | solution.py:72
  5.8 3.4 %collective-permute-start.2 = (f32[1536,512]{1,0:T(8,128)}, f32[1536,512]{1,0:T(8,128)}, u32[]{:S(2)}, u32[]{:S(2)}) collective-permute-start(f32[1536,512]{1,0:T(8,128)} %slice.165), channel_id=1, source_target_pairs={{2,0},{3,1},{4,2},{5,3},{6,4},{7,5},{10,8},{11,9},{12,10},{13,11},... | collective-permute-start | bytes 9437192 | tf_op jit(solution)/shard_map/ppermute | solution.py:17
  9.2 3.2 %reduce_sum.18 = f32[1024]{0:T(1024)S(1)} reduce(f32[1536,1024]{1,0:T(8,128)} %param.2, f32[]{:T(128)} %constant.224.clone.1), dimensions={0}, to_apply=%region_0.0 | reduce | flops 1571840 | bytes 6295556 | tf_op jit(solution)/shard_map/reduce_sum | solution.py:74
  12.4 18.5 %psum.28 = f32[1024]{0:T(1024)S(1)} all-reduce(f32[1024]{0:T(1024)S(1)} %reduce_sum.18), channel_id=1, replica_groups=mesh['samp_x'=4,'samp_z'=8,'snp'=8] {'samp_z'}, use_global_device_ids=true, to_apply=%region_1.0 | all-reduce | flops 1024 | bytes 8192 | tf_op jit(solution)/shard_map/psum | solution.py:54
  30.9 10.5 %psum.29 = f32[1024]{0:T(1024)S(1)} all-reduce(f32[1024]{0:T(1024)S(1)} %psum.28), channel_id=1, replica_groups=mesh['samp_x'=4,'samp_z'=8,'snp'=8] {'samp_x'}, use_global_device_ids=true, to_apply=%region_2.0 | all-reduce | flops 1024 | bytes 8192 | tf_op jit(solution)/shard_map/psum | solution.py:54
  41.4 6.6 %multiply_reduce_fusion = (f32[1024]{0:T(1024)S(1)}, f32[1536,1024]{1,0:T(8,128)}) fusion(f32[1536,1024]{1,0:T(8,128)} %param.2, f32[1024]{0:T(1024)S(1)} %broadcast_multiply_fusion), kind=kLoop, calls=%fused_computation.1 | loop fusion | flops 4717568 | bytes 12591104 | tf_op jit(solution)/shard_map/reduce_sum | solution.py:77
  48.0 14.1 %psum.30 = f32[1024]{0:T(1024)S(1)} all-reduce(f32[1024]{0:T(1024)S(1)} %get-tuple-element.45), channel_id=1, replica_groups=mesh['samp_x'=4,'samp_z'=8,'snp'=8] {'samp_z'}, use_global_device_ids=true, to_apply=%region_4.0 | all-reduce | flops 1024 | bytes 8192 | tf_op jit(solution)/shard_map/psum | solution.py:54
  62.1 7.7 %psum.31 = f32[1024]{0:T(1024)S(1)} all-reduce(f32[1024]{0:T(1024)S(1)} %psum.30), channel_id=1, replica_groups=mesh['samp_x'=4,'samp_z'=8,'snp'=8] {'samp_x'}, use_global_device_ids=true, to_apply=%region_5.0 | all-reduce | flops 1024 | bytes 8192 | tf_op jit(solution)/shard_map/psum | solution.py:54
  69.9 1.9 collective-permute-start.1
  71.8 2.1 collective-permute-start.3
  74.1 5.6 %fusion.14 = f32[512,512]{1,0:T(8,128)S(1)} fusion(f32[1536,1024]{1,0:T(8,128)} %get-tuple-element.46), kind=kOutput, calls=%fused_computation.18 | convolution fusion | flops 2415919104 | bytes 4194304 | tf_op jit(solution)/shard_map/dot_general | solution.py:96
  79.7 5.5 %fusion.19 = f32[512,512]{1,0:T(8,128)S(1)} fusion(f32[1536,1024]{1,0:T(8,128)} %get-tuple-element.46), kind=kOutput, calls=%fused_computation.23 | convolution fusion | flops 2415919104 | bytes 4194304 | tf_op jit(solution)/shard_map/dot_general | solution.py:96
  85.2 2.8 fusion.12
  88.1 52.1 %collective-permute-done.3 = f32[2,512]{1,0:T(2,128)S(1)} collective-permute-done((f32[2,512]{1,0:T(2,128)S(1)}, f32[2,512]{1,0:T(2,128)S(1)}, u32[]{:S(2)}, u32[]{:S(2)}) %collective-permute-start.3) | collective-permute-done | bytes 4128 | tf_op jit(solution)/shard_map/ppermute | solution.py:17
  140.3 5.6 %fusion = f32[512,512]{1,0:T(8,128)S(1)} fusion(f32[1536,512]{1,0:T(8,128)} %collective-permute-done.2, f32[1536,1024]{1,0:T(8,128)} %get-tuple-element.46, f32[512]{0:T(512)S(1)} %bitcast.157), kind=kOutput, calls=%fused_computation.2 | convolution fusion | flops 2416705536 | bytes 7342080 | tf_op jit(solution)/shard_map/dot_general | solution.py:96
  145.9 3.9 %broadcast_subtract_fusion = f32[1536,1024]{1,0:T(8,128)S(1)} fusion(f32[1536,1024]{1,0:T(8,128)} %collective-permute-done, f32[1024]{0:T(1024)S(1)} %bitcast.153), kind=kLoop, calls=%fused_computation.4 | loop fusion | flops 1572864 | bytes 12587008 | tf_op jit(solution)/shard_map/sub | solution.py:88
  149.8 2.7 fusion.4
  152.6 2.7 fusion.6
  155.3 2.7 fusion.2
  158.1 2.7 fusion.8
  160.9 4.5 %maximum_select_fusion = f32[4,8,16,2,4,512]{5,2,4,3,1,0:T(8,128)} fusion(f32[4,8,16,1,1,512]{5,2,4,3,1,0:T(8,128)S(1)} %bitcast.146, f32[4,8,16,1,1,512]{5,2,4,3,1,0:T(8,128)S(1)} %bitcast.144, f32[4,8,16,1,1,512]{5,2,4,3,1,0:T(8,128)S(1)} %bitcast.143, f32[4,8,16,1,1,512]{5,2,4,3,1,0:T(8,128)S(1)} %bitcast.148, f32[4,8,16,1,1,512]{5,2,4,3,1,0:T(8,128)S(1)} %bitcast.142, ...), kind=kLoop, calls=%fused_computation | loop fusion | flops 16777216 | bytes 16777224 | tf_op jit(solution)/shard_map/jit(_where)/select_n | solution.py:111
  165.3 10.3 %dynamic-slice_bitcast_fusion = (f32[4,16,2,4,512]{4,1,3,2,0:T(8,128)S(1)}, f32[4,16,2,4,512]{4,1,3,2,0:T(8,128)S(1)}, f32[4,16,2,4,512]{4,1,3,2,0:T(8,128)}, f3...) fusion(f32[4,8,16,2,4,512]{5,2,4,3,1,0:T(8,128)} %maximum_selec, ...), kind=kLoop, calls=%fused_computation.39 | loop fusion | bytes 29360184 | tf_op jit(solution)/shard_map/jit(dynamic_index_in_dim)/squeeze | solution.py:27
  176.9 5.9 %collective-permute-start.5 = (f32[4,16,2,4,256]{4,1,3,2,0:T(8,128)S(1)}, f32[4,16,2,4,256]{4,1,3,2,0:T(8,128)S(1)}, u32[]{:S(2)}, u32[]{:S(2)}) collective-permute-start(f32[4,16,2,4,256]{4,1,3,2,0:T(8,128)S(1)} %slice.217), channel_id=1, source_target_pairs={{0,56},{8,0},{16,8},{24,16},{32,24},{40,32},{48,40},{56,48},{1,57}... | collective-permute-start | bytes 1572872 | tf_op jit(solution)/shard_map/ppermute | solution.py:35
  182.9 11.4 %collective-permute-done.5 = f32[4,16,2,4,256]{4,1,3,2,0:T(8,128)S(1)} collective-permute-done((f32[4,16,2,4,256]{4,1,3,2,0:T(8,128)S(1)}, f32[4,16,2,4,256]{4,1,3,2,0:T(8,128)S(1)}, u32[]{:S(2)}, u32[]{:S(2)}) %collective-permute-start.5) | collective-permute-done | bytes 524320 | tf_op jit(solution)/shard_map/ppermute | solution.py:35
  195.5 2.2 collective-permute-done.4
  198.9 1.6 collective-permute-start.7
  201.0 10.7 %collective-permute-done.7 = f32[4,16,2,4,256]{4,1,3,2,0:T(8,128)S(1)} collective-permute-done((f32[4,16,2,4,256]{4,1,3,2,0:T(8,128)S(1)}, f32[4,16,2,4,256]{4,1,3,2,0:T(8,128)S(1)}, u32[]{:S(2)}, u32[]{:S(2)}) %collective-permute-start.7) | collective-permute-done | bytes 524320 | tf_op jit(solution)/shard_map/ppermute | solution.py:35
  212.9 1.6 collective-permute-done.6
  216.7 9.9 %collective-permute-done.9 = f32[4,16,2,4,256]{4,1,3,2,0:T(8,128)S(1)} collective-permute-done((f32[4,16,2,4,256]{4,1,3,2,0:T(8,128)S(1)}, f32[4,16,2,4,256]{4,1,3,2,0:T(8,128)S(1)}, u32[]{:S(2)}, u32[]{:S(2)}) %collective-permute-start.9) | collective-permute-done | bytes 524320 | tf_op jit(solution)/shard_map/ppermute | solution.py:35
  226.7 2.5 collective-permute-done.8
  229.8 1.6 collective-permute-start.10
  231.4 9.0 %collective-permute-done.11 = f32[4,16,2,4,256]{4,1,3,2,0:T(8,128)S(1)} collective-permute-done((f32[4,16,2,4,256]{4,1,3,2,0:T(8,128)S(1)}, f32[4,16,2,4,256]{4,1,3,2,0:T(8,128)S(1)}, u32[]{:S(2)}, u32[]{:S(2)}) %collective-permute-start.11) | collective-permute-done | bytes 524320 | tf_op jit(solution)/shard_map/ppermute | solution.py:35
  240.5 1.5 collective-permute-done.10
  242.6 1.6 collective-permute-start.12
  244.2 8.3 %collective-permute-done.13 = f32[4,16,2,4,256]{4,1,3,2,0:T(8,128)S(1)} collective-permute-done((f32[4,16,2,4,256]{4,1,3,2,0:T(8,128)S(1)}, f32[4,16,2,4,256]{4,1,3,2,0:T(8,128)S(1)}, u32[]{:S(2)}, u32[]{:S(2)}) %collective-permute-start.13) | collective-permute-done | bytes 524320 | tf_op jit(solution)/shard_map/ppermute | solution.py:35
  254.7 1.7 collective-permute-start.14
  256.4 8.0 %collective-permute-done.15 = f32[4,16,2,4,256]{4,1,3,2,0:T(8,128)S(1)} collective-permute-done((f32[4,16,2,4,256]{4,1,3,2,0:T(8,128)S(1)}, f32[4,16,2,4,256]{4,1,3,2,0:T(8,128)S(1)}, u32[]{:S(2)}, u32[]{:S(2)}) %collective-permute-start.15) | collective-permute-done | bytes 524320 | tf_op jit(solution)/shard_map/ppermute | solution.py:35
  266.9 1.5 collective-permute-start.16
  268.4 1.8 collective-permute-start.17
  270.2 7.2 %collective-permute-done.16 = f32[4,16,2,4,256]{4,1,3,2,0:T(8,128)S(1)} collective-permute-done((f32[4,16,2,4,256]{4,1,3,2,0:T(8,128)S(1)}, f32[4,16,2,4,256]{4,1,3,2,0:T(8,128)S(1)}, u32[]{:S(2)}, u32[]{:S(2)}) %collective-permute-start.16) | collective-permute-done | bytes 524320 | tf_op jit(solution)/shard_map/ppermute | solution.py:34
  278.1 2.8 collective-permute-start.19
  281.0 3.2 %collective-permute-done.19 = f32[16,2,4,256]{3,0,2,1:T(8,128)S(1)} collective-permute-done((f32[16,2,4,256]{3,0,2,1:T(8,128)S(1)}, f32[16,2,4,256]{3,0,2,1:T(8,128)S(1)}, u32[]{:S(2)}, u32[]{:S(2)}) %collective-permute-start.19) | collective-permute-done | bytes 131104 | tf_op jit(solution)/shard_map/ppermute | solution.py:35
  284.2 2.9 collective-permute-done.18
  287.4 2.0 collective-permute-start.20
  289.4 2.8 collective-permute-done.21
  294.5 2.5 collective-permute-start.23
  296.9 2.9 collective-permute-done.22
  (79 shorter events, 18.0 us)
Async XLA Ops:
  0.0 145.9 %collective-permute-start = (f32[1536,1024]{1,0:T(8,128)}, f32[1536,1024]{1,0:T(8,128)}, u32[]{:S(2)}, u32[]{:S(2)}) collective-permute-start(f32[1536,1024]{1,0:T(8,128)} %param.2), channel_id=1, source_target_pairs={{1,0},{2,1},{3,2},{4,3},{5,4},{6,5},{7,6},{9,8},{10,9},{11,10},{12... | collective-permute-start | bytes 18874376 | tf_op jit(solution)/shard_map/ppermute | solution.py:17
  5.8 134.5 %collective-permute-start.2 = (f32[1536,512]{1,0:T(8,128)}, f32[1536,512]{1,0:T(8,128)}, u32[]{:S(2)}, u32[]{:S(2)}) collective-permute-start(f32[1536,512]{1,0:T(8,128)} %slice.165), channel_id=1, source_target_pairs={{2,0},{3,1},{4,2},{5,3},{6,4},{7,5},{10,8},{11,9},{12,10},{13,11},... | collective-permute-start | bytes 9437192 | tf_op jit(solution)/shard_map/ppermute | solution.py:17
  41.4 32.7 %copy-start.8 = (s32[2]{0:T(128)S(1)}, s32[2]{0:T(128)}, u32[]{:S(2)}) copy-start(s32[2]{0:T(128)} %param.3) | copy-start | bytes 28
  69.9 70.4 %collective-permute-start.1 = (f32[2,1024]{1,0:T(2,128)S(1)}, f32[2,1024]{1,0:T(2,128)S(1)}, u32[]{:S(2)}, u32[]{:S(2)}) collective-permute-start(f32[2,1024]{1,0:T(2,128)S(1)} %pad_maximum_fusion.2), channel_id=1, source_target_pairs={{1,0},{2,1},{3,2},{4,3},{5,4},{6,5},{7,6},{9,8},{10,9},{11,10},{12... | collective-permute-start | bytes 24584 | tf_op jit(solution)/shard_map/ppermute | solution.py:17
  71.8 68.4 %collective-permute-start.3 = (f32[2,512]{1,0:T(2,128)S(1)}, f32[2,512]{1,0:T(2,128)S(1)}, u32[]{:S(2)}, u32[]{:S(2)}) collective-permute-start(f32[2,512]{1,0:T(2,128)S(1)} %fusion.74), channel_id=1, source_target_pairs={{2,0},{3,1},{4,2},{5,3},{6,4},{7,5},{10,8},{11,9},{12,10},{13,11},... | collective-permute-start | bytes 12296 | tf_op jit(solution)/shard_map/ppermute | solution.py:17
  74.0 11.2 %copy-start = (f32[1536,1024]{1,0:T(8,128)S(1)}, f32[1536,1024]{1,0:T(8,128)}, u32[]{:S(2)}) copy-start(f32[1536,1024]{1,0:T(8,128)} %get-tuple-element.46) | copy-start | bytes 18874372
  140.3 9.6 %slice-start = ((s8[6291456]{0:T(1024)(128)(4,1)}), s8[4194304]{0:T(1024)(128)(4,1)S(1)}, s32[]{:S(2)}) async-start(s8[6291456]{0:T(1024)(128)(4,1)} %bitcast.139), calls=%async_computation | async-start | bytes 8388608
  145.9 3.9 %slice-start.1 = ((s8[6291456]{0:T(1024)(128)(4,1)}), s8[2097152]{0:T(1024)(128)(4,1)S(1)}, s32[]{:S(2)}) async-start(s8[6291456]{0:T(1024)(128)(4,1)} %bitcast.139), calls=%async_computation.1 | async-start | bytes 4194304
  175.6 38.9 %copy-start.7 = (f32[4,16,2,4,512]{4,1,3,2,0:T(8,128)S(1)}, f32[4,16,2,4,512]{4,1,3,2,0:T(8,128)}, u32[]{:S(2)}) copy-start(f32[4,16,2,4,512]{4,1,3,2,0:T(8,128)} %get-tuple-element.56) | copy-start | bytes 3145732
  175.6 50.9 %copy-start.6 = (f32[4,16,2,4,512]{4,1,3,2,0:T(8,128)S(1)}, f32[4,16,2,4,512]{4,1,3,2,0:T(8,128)}, u32[]{:S(2)}) copy-start(f32[4,16,2,4,512]{4,1,3,2,0:T(8,128)} %get-tuple-element.53) | copy-start | bytes 3145732
  175.6 53.6 %copy-start.5 = (f32[4,16,2,4,512]{4,1,3,2,0:T(8,128)S(1)}, f32[4,16,2,4,512]{4,1,3,2,0:T(8,128)}, u32[]{:S(2)}) copy-start(f32[4,16,2,4,512]{4,1,3,2,0:T(8,128)} %get-tuple-element.54) | copy-start | bytes 3145732
  175.6 64.8 %copy-start.4 = (f32[4,16,2,4,512]{4,1,3,2,0:T(8,128)S(1)}, f32[4,16,2,4,512]{4,1,3,2,0:T(8,128)}, u32[]{:S(2)}) copy-start(f32[4,16,2,4,512]{4,1,3,2,0:T(8,128)} %get-tuple-element.51) | copy-start | bytes 3145732
  175.7 66.3 %copy-start.3 = (f32[4,16,2,4,512]{4,1,3,2,0:T(8,128)S(1)}, f32[4,16,2,4,512]{4,1,3,2,0:T(8,128)}, u32[]{:S(2)}) copy-start(f32[4,16,2,4,512]{4,1,3,2,0:T(8,128)} %get-tuple-element.52) | copy-start | bytes 3145732
  176.9 17.3 %collective-permute-start.5 = (f32[4,16,2,4,256]{4,1,3,2,0:T(8,128)S(1)}, f32[4,16,2,4,256]{4,1,3,2,0:T(8,128)S(1)}, u32[]{:S(2)}, u32[]{:S(2)}) collective-permute-start(f32[4,16,2,4,256]{4,1,3,2,0:T(8,128)S(1)} %slice.217), channel_id=1, source_target_pairs={{0,56},{8,0},{16,8},{24,16},{32,24},{40,32},{48,40},{56,48},{1,57}... | collective-permute-start | bytes 1572872 | tf_op jit(solution)/shard_map/ppermute | solution.py:35
  182.9 14.8 %collective-permute-start.4 = (f32[4,16,2,4,256]{4,1,3,2,0:T(8,128)S(1)}, f32[4,16,2,4,256]{4,1,3,2,0:T(8,128)S(1)}, u32[]{:S(2)}, u32[]{:S(2)}) collective-permute-start(f32[4,16,2,4,256]{4,1,3,2,0:T(8,128)S(1)} %slice.216), channel_id=1, source_target_pairs={{0,8},{8,16},{16,24},{24,32},{32,40},{40,48},{48,56},{56,0},{1,9},... | collective-permute-start | bytes 1572872 | tf_op jit(solution)/shard_map/ppermute | solution.py:34
  194.3 58.2 %copy-start.2 = (f32[4,16,2,4,512]{4,1,3,2,0:T(8,128)S(1)}, f32[4,16,2,4,512]{4,1,3,2,0:T(8,128)}, u32[]{:S(2)}) copy-start(f32[4,16,2,4,512]{4,1,3,2,0:T(8,128)} %get-tuple-element.49) | copy-start | bytes 3145732
  197.7 56.3 %copy-start.1 = (f32[4,16,2,4,512]{4,1,3,2,0:T(8,128)S(1)}, f32[4,16,2,4,512]{4,1,3,2,0:T(8,128)}, u32[]{:S(2)}) copy-start(f32[4,16,2,4,512]{4,1,3,2,0:T(8,128)} %get-tuple-element.50) | copy-start | bytes 3145732
  198.9 12.8 %collective-permute-start.7 = (f32[4,16,2,4,256]{4,1,3,2,0:T(8,128)S(1)}, f32[4,16,2,4,256]{4,1,3,2,0:T(8,128)S(1)}, u32[]{:S(2)}, u32[]{:S(2)}) collective-permute-start(f32[4,16,2,4,256]{4,1,3,2,0:T(8,128)S(1)} %slice_add_fusion.12), channel_id=1, source_target_pairs={{0,56},{8,0},{16,8},{24,16},{32,24},{40,32},{48,40},{56,48},{1,57}... | collective-permute-start | bytes 1572872 | tf_op jit(solution)/shard_map/ppermute | solution.py:35
  200.5 14.0 %collective-permute-start.6 = (f32[4,16,2,4,256]{4,1,3,2,0:T(8,128)S(1)}, f32[4,16,2,4,256]{4,1,3,2,0:T(8,128)S(1)}, u32[]{:S(2)}, u32[]{:S(2)}) collective-permute-start(f32[4,16,2,4,256]{4,1,3,2,0:T(8,128)S(1)} %slice_add_fusion.13), channel_id=1, source_target_pairs={{0,8},{8,16},{16,24},{24,32},{32,40},{40,48},{48,56},{56,0},{1,9},... | collective-permute-start | bytes 1572872 | tf_op jit(solution)/shard_map/ppermute | solution.py:34
  214.6 12.0 %collective-permute-start.9 = (f32[4,16,2,4,256]{4,1,3,2,0:T(8,128)S(1)}, f32[4,16,2,4,256]{4,1,3,2,0:T(8,128)S(1)}, u32[]{:S(2)}, u32[]{:S(2)}) collective-permute-start(f32[4,16,2,4,256]{4,1,3,2,0:T(8,128)S(1)} %slice_add_fusion.10), channel_id=1, source_target_pairs={{0,56},{8,0},{16,8},{24,16},{32,24},{40,32},{48,40},{56,48},{1,57}... | collective-permute-start | bytes 1572872 | tf_op jit(solution)/shard_map/ppermute | solution.py:35
  216.1 13.1 %collective-permute-start.8 = (f32[4,16,2,4,256]{4,1,3,2,0:T(8,128)S(1)}, f32[4,16,2,4,256]{4,1,3,2,0:T(8,128)S(1)}, u32[]{:S(2)}, u32[]{:S(2)}) collective-permute-start(f32[4,16,2,4,256]{4,1,3,2,0:T(8,128)S(1)} %slice_add_fusion.11), channel_id=1, source_target_pairs={{0,8},{8,16},{16,24},{24,32},{32,40},{40,48},{48,56},{56,0},{1,9},... | collective-permute-start | bytes 1572872 | tf_op jit(solution)/shard_map/ppermute | solution.py:34
  229.3 11.1 %collective-permute-start.11 = (f32[4,16,2,4,256]{4,1,3,2,0:T(8,128)S(1)}, f32[4,16,2,4,256]{4,1,3,2,0:T(8,128)S(1)}, u32[]{:S(2)}, u32[]{:S(2)}) collective-permute-start(f32[4,16,2,4,256]{4,1,3,2,0:T(8,128)S(1)} %slice_add_fusion.8), channel_id=1, source_target_pairs={{0,56},{8,0},{16,8},{24,16},{32,24},{40,32},{48,40},{56,48},{1,57}... | collective-permute-start | bytes 1572872 | tf_op jit(solution)/shard_map/ppermute | solution.py:35
  229.8 12.3 %collective-permute-start.10 = (f32[4,16,2,4,256]{4,1,3,2,0:T(8,128)S(1)}, f32[4,16,2,4,256]{4,1,3,2,0:T(8,128)S(1)}, u32[]{:S(2)}, u32[]{:S(2)}) collective-permute-start(f32[4,16,2,4,256]{4,1,3,2,0:T(8,128)S(1)} %slice_add_fusion.9), channel_id=1, source_target_pairs={{0,8},{8,16},{16,24},{24,32},{32,40},{40,48},{48,56},{56,0},{1,9},... | collective-permute-start | bytes 1572872 | tf_op jit(solution)/shard_map/ppermute | solution.py:34
  242.1 10.4 %collective-permute-start.13 = (f32[4,16,2,4,256]{4,1,3,2,0:T(8,128)S(1)}, f32[4,16,2,4,256]{4,1,3,2,0:T(8,128)S(1)}, u32[]{:S(2)}, u32[]{:S(2)}) collective-permute-start(f32[4,16,2,4,256]{4,1,3,2,0:T(8,128)S(1)} %slice_add_fusion.6), channel_id=1, source_target_pairs={{0,56},{8,0},{16,8},{24,16},{32,24},{40,32},{48,40},{56,48},{1,57}... | collective-permute-start | bytes 1572872 | tf_op jit(solution)/shard_map/ppermute | solution.py:35
  242.6 11.4 %collective-permute-start.12 = (f32[4,16,2,4,256]{4,1,3,2,0:T(8,128)S(1)}, f32[4,16,2,4,256]{4,1,3,2,0:T(8,128)S(1)}, u32[]{:S(2)}, u32[]{:S(2)}) collective-permute-start(f32[4,16,2,4,256]{4,1,3,2,0:T(8,128)S(1)} %slice_add_fusion.7), channel_id=1, source_target_pairs={{0,8},{8,16},{16,24},{24,32},{32,40},{40,48},{48,56},{56,0},{1,9},... | collective-permute-start | bytes 1572872 | tf_op jit(solution)/shard_map/ppermute | solution.py:34
  254.1 10.3 %collective-permute-start.15 = (f32[4,16,2,4,256]{4,1,3,2,0:T(8,128)S(1)}, f32[4,16,2,4,256]{4,1,3,2,0:T(8,128)S(1)}, u32[]{:S(2)}, u32[]{:S(2)}) collective-permute-start(f32[4,16,2,4,256]{4,1,3,2,0:T(8,128)S(1)} %slice_add_fusion.4), channel_id=1, source_target_pairs={{0,56},{8,0},{16,8},{24,16},{32,24},{40,32},{48,40},{56,48},{1,57}... | collective-permute-start | bytes 1572872 | tf_op jit(solution)/shard_map/ppermute | solution.py:35
  254.7 12.1 %collective-permute-start.14 = (f32[4,16,2,4,256]{4,1,3,2,0:T(8,128)S(1)}, f32[4,16,2,4,256]{4,1,3,2,0:T(8,128)S(1)}, u32[]{:S(2)}, u32[]{:S(2)}) collective-permute-start(f32[4,16,2,4,256]{4,1,3,2,0:T(8,128)S(1)} %slice_add_fusion.5), channel_id=1, source_target_pairs={{0,8},{8,16},{16,24},{24,32},{32,40},{40,48},{48,56},{56,0},{1,9},... | collective-permute-start | bytes 1572872 | tf_op jit(solution)/shard_map/ppermute | solution.py:34
  266.9 10.5 %collective-permute-start.16 = (f32[4,16,2,4,256]{4,1,3,2,0:T(8,128)S(1)}, f32[4,16,2,4,256]{4,1,3,2,0:T(8,128)S(1)}, u32[]{:S(2)}, u32[]{:S(2)}) collective-permute-start(f32[4,16,2,4,256]{4,1,3,2,0:T(8,128)S(1)} %slice_add_fusion.3), channel_id=1, source_target_pairs={{0,8},{8,16},{16,24},{24,32},{32,40},{40,48},{48,56},{56,0},{1,9},... | collective-permute-start | bytes 1572872 | tf_op jit(solution)/shard_map/ppermute | solution.py:34
  268.4 9.4 %collective-permute-start.17 = (f32[4,16,2,4,256]{4,1,3,2,0:T(8,128)}, f32[4,16,2,4,256]{4,1,3,2,0:T(8,128)S(1)}, u32[]{:S(2)}, u32[]{:S(2)}) collective-permute-start(f32[4,16,2,4,256]{4,1,3,2,0:T(8,128)} %slice_add_fusion.2), channel_id=1, source_target_pairs={{0,56},{8,0},{16,8},{24,16},{32,24},{40,32},{48,40},{56,48},{1,57}... | collective-permute-start | bytes 1572872 | tf_op jit(solution)/shard_map/ppermute | solution.py:35
  278.1 6.1 %collective-permute-start.19 = (f32[16,2,4,256]{3,0,2,1:T(8,128)S(1)}, f32[16,2,4,256]{3,0,2,1:T(8,128)S(1)}, u32[]{:S(2)}, u32[]{:S(2)}) collective-permute-start(f32[16,2,4,256]{3,0,2,1:T(8,128)S(1)} %slice.233), channel_id=1, source_target_pairs={{0,192},{64,0},{128,64},{192,128},{1,193},{65,1},{129,65},{193,129... | collective-permute-start | bytes 393224 | tf_op jit(solution)/shard_map/ppermute | solution.py:35
  281.0 6.2 %collective-permute-start.18 = (f32[16,2,4,256]{3,0,2,1:T(8,128)S(1)}, f32[16,2,4,256]{3,0,2,1:T(8,128)S(1)}, u32[]{:S(2)}, u32[]{:S(2)}) collective-permute-start(f32[16,2,4,256]{3,0,2,1:T(8,128)S(1)} %slice.232), channel_id=1, source_target_pairs={{0,64},{64,128},{128,192},{192,0},{1,65},{65,129},{129,193},{193,1... | collective-permute-start | bytes 393224 | tf_op jit(solution)/shard_map/ppermute | solution.py:34
  287.2 5.0 %collective-permute-start.21 = (f32[16,2,4,256]{3,0,2,1:T(8,128)S(1)}, f32[16,2,4,256]{3,0,2,1:T(8,128)S(1)}, u32[]{:S(2)}, u32[]{:S(2)}) collective-permute-start(f32[16,2,4,256]{3,0,2,1:T(8,128)S(1)} %slice_add_fusion.18), channel_id=1, source_target_pairs={{0,192},{64,0},{128,64},{192,128},{1,193},{65,1},{129,65},{193,129... | collective-permute-start | bytes 393224 | tf_op jit(solution)/shard_map/ppermute | solution.py:35
  287.4 6.2 %collective-permute-start.20 = (f32[16,2,4,256]{3,0,2,1:T(8,128)S(1)}, f32[16,2,4,256]{3,0,2,1:T(8,128)S(1)}, u32[]{:S(2)}, u32[]{:S(2)}) collective-permute-start(f32[16,2,4,256]{3,0,2,1:T(8,128)S(1)} %slice_add_fusion.19), channel_id=1, source_target_pairs={{0,64},{64,128},{128,192},{192,0},{1,65},{65,129},{129,193},{193,1... | collective-permute-start | bytes 393224 | tf_op jit(solution)/shard_map/ppermute | solution.py:34
  293.6 6.3 %collective-permute-start.22 = (f32[16,2,4,256]{3,0,2,1:T(8,128)S(1)}, f32[16,2,4,256]{3,0,2,1:T(8,128)S(1)}, u32[]{:S(2)}, u32[]{:S(2)}) collective-permute-start(f32[16,2,4,256]{3,0,2,1:T(8,128)S(1)} %slice_add_fusion.17), channel_id=1, source_target_pairs={{0,64},{64,128},{128,192},{192,0},{1,65},{65,129},{129,193},{193,1... | collective-permute-start | bytes 393224 | tf_op jit(solution)/shard_map/ppermute | solution.py:34
  294.5 5.4 %collective-permute-start.23 = (f32[16,2,4,256]{3,0,2,1:T(8,128)S(1)}, f32[16,2,4,256]{3,0,2,1:T(8,128)S(1)}, u32[]{:S(2)}, u32[]{:S(2)}) collective-permute-start(f32[16,2,4,256]{3,0,2,1:T(8,128)S(1)} %slice_add_fusion.16), channel_id=1, source_target_pairs={{0,192},{64,0},{128,64},{192,128},{1,193},{65,1},{129,65},{193,129... | collective-permute-start | bytes 393224 | tf_op jit(solution)/shard_map/ppermute | solution.py:35
